TPU v7x, 128 devices: a whole 4x4x4 slice. The times are simulated.
128 devices in a mesh: lon: 32 (over z_lo, y, x), lat: 4 (over z_hi, core).
Axes of the slice: x: 4, y: 4, z: 4 (z_hi: 2, z_lo: 2; z = z_hi * 2 + z_lo), core: 2. Of those that a mesh axis runs over, the one named last changes fastest.
Arguments:
- increment: float32 [3, 8192, 1024], P(None, 'lon', 'lat'), may hold values from -6 to 6
- depth_field: float32 [8192, 1024], P('lon', 'lat'), may hold values from 0.5 to 1.5
- coriolis: float32 [1024], P('lat'), may hold values from -0.5 to 0.5
- footprint: bfloat16 [128, 128], replicated, may hold values from -0.5 to 0.5
- channel_weights: float32 [5, 3], replicated, may hold values from -3.5 to 3.5
- track_tiles: int32 [2, 4, 32, 32], P(None, 'lat', 'lon'), may hold values from -1 to 3, as said below
- innovations: bfloat16 [2, 4, 32, 32, 5, 128, 128], P(None, 'lat', 'lon'), may hold values from -6 to 6
- obs_weights: bfloat16 [2, 4, 32, 32], P(None, 'lat', 'lon'), may hold values from 0.25 to 2
Outputs:
- gradient: float32 [3, 8192, 1024], P(None, 'lon', 'lat')
Inputs may be any that keep to these rules, and one draw needn't show every extreme that they name: `track_tiles`: tiles are numbered 0 to 3 within a slab's block of a band. At every observation time, in every band, one owner observes a tile of every slab; other entries are -1 or a tile.
All inputs are finite; a program needn't handle non-finite values.
Results may differ from a plain program's by a relative error of at most 0.0028.
Values may be sent and summed in bfloat16 or wider, within the bound.
No kernel may reach another device: no remote copies, remote signals or barrier semaphores. Data moves between devices by JAX's collectives and lax.ppermute only.
A program may use at most 192 MiB of HBM per device.

v0:
```python
import jax
import jax.numpy as jnp
from jax import lax
from jax.sharding import PartitionSpec as P
from jax.experimental import pallas as pl
from jax.experimental.pallas import tpu as pltpu

TILE = 128
STEPS = 6
OBS_TIMES = 2
HALO = 2 * STEPS
OWNERS_STEP = 4


COURANT = 0.7


def extend_lon(x, width):
    peers, length = lax.axis_size("lon"), x.shape[-2]
    up = [(i, (i + 1) % peers) for i in range(peers)]
    down = [(j, i) for i, j in up]
    before = lax.ppermute(x[..., length - width :, :], "lon", up)
    after = lax.ppermute(x[..., :width, :], "lon", down)
    return jnp.concatenate([before, x, after], axis=-2)


def extend_lat(x, width):
    peers, length = lax.axis_size("lat"), x.shape[-1]
    up = [(i, i + 1) for i in range(peers - 1)]
    down = [(j, i) for i, j in up]
    before = lax.ppermute(x[..., length - width :], "lat", up)
    after = lax.ppermute(x[..., :width], "lat", down)
    return jnp.concatenate([before, x, after], axis=-1)


def extend(x, width):
    return extend_lat(extend_lon(x, width), width)


def lon_diff(values):
    return 0.5 * (jnp.roll(values, -1, axis=0) - jnp.roll(values, 1, axis=0))


def lat_diff(values):
    return 0.5 * (jnp.roll(values, -1, axis=1) - jnp.roll(values, 1, axis=1))


def tangent_step(east_wind, north_wind, height, depth_field, coriolis, inside):
    height_next = height - COURANT * (
        lon_diff(depth_field * east_wind) + lat_diff(depth_field * north_wind)
    )
    height_next = jnp.where(inside, height_next, 0.0)
    east_next = east_wind + coriolis * north_wind - COURANT * lon_diff(height_next)
    north_next = north_wind - coriolis * east_next - COURANT * lat_diff(height_next)
    north_next = jnp.where(inside, north_next, 0.0)
    return (east_next, north_next, height_next)


def adjoint_step(east_adj, north_adj, height_adj, depth_field, coriolis, inside):
    east_once = east_adj - coriolis * north_adj
    height_once = height_adj + COURANT * (lat_diff(north_adj) + lon_diff(east_once))
    height_once = jnp.where(inside, height_once, 0.0)
    east_prev = east_once + COURANT * depth_field * lon_diff(height_once)
    north_prev = north_adj + coriolis * east_once + COURANT * depth_field * lat_diff(height_once)
    north_prev = jnp.where(inside, north_prev, 0.0)
    return (east_prev, north_prev, height_once)


def to_tiles(block_data):
    fields, row_total, col_total = block_data.shape
    blocks = block_data.reshape(fields, row_total // TILE, TILE, col_total // TILE, TILE)
    return blocks.transpose(1, 3, 0, 2, 4).reshape(-1, fields, TILE, TILE)


def from_tiles(pieces, row_total, col_total):
    fields = pieces.shape[1]
    blocks = pieces.reshape(row_total // TILE, col_total // TILE, fields, TILE, TILE)
    return blocks.transpose(2, 0, 3, 1, 4).reshape(fields, row_total, col_total)


def residual_kernel(index_ref, valid_ref, scale_ref, weight_ref, spread_ref, innov_ref, out_ref, radiance_ref):
    step = pl.program_id(0)
    tiles, fields = spread_ref.shape[0], spread_ref.shape[1]
    channels = radiance_ref.shape[1]

    @pl.when(step == 0)
    def _():
        for j in range(tiles):
            for h in range(channels):
                acc = weight_ref[h * fields] * spread_ref[j, 0]
                for c in range(1, fields):
                    acc = acc + weight_ref[h * fields + c] * spread_ref[j, c]
                radiance_ref[j, h] = acc
        out_ref[...] = jnp.zeros_like(out_ref)

    for k in range(OWNERS_STEP):
        owner = step * OWNERS_STEP + k
        j = index_ref[owner]
        scale = scale_ref[owner]

        @pl.when(valid_ref[owner] != 0)
        def _():
            weighted = [
                scale * (radiance_ref[j, h] - innov_ref[k, h].astype(jnp.float32))
                for h in range(channels)
            ]
            for c in range(fields):
                mixed = weight_ref[c] * weighted[0]
                for h in range(1, channels):
                    mixed = mixed + weight_ref[h * fields + c] * weighted[h]
                out_ref[j, c] = out_ref[j, c] + mixed.astype(jnp.bfloat16).astype(jnp.float32)


def residual_sums(spread, innov, index, valid, scale, channel_weights):
    tiles, fields = spread.shape[0], spread.shape[1]
    owners, channels = innov.shape[0], innov.shape[1]
    smem = pl.BlockSpec(memory_space=pltpu.SMEM)
    return pl.pallas_call(
        residual_kernel,
        grid=(owners // OWNERS_STEP,),
        in_specs=[
            smem,
            smem,
            smem,
            smem,
            pl.BlockSpec(spread.shape, lambda s: (0, 0, 0, 0)),
            pl.BlockSpec((OWNERS_STEP,) + innov.shape[1:], lambda s: (s, 0, 0, 0)),
        ],
        out_specs=pl.BlockSpec(spread.shape, lambda s: (0, 0, 0, 0)),
        out_shape=jax.ShapeDtypeStruct(spread.shape, jnp.float32),
        scratch_shapes=[pltpu.VMEM((tiles, channels) + spread.shape[2:], jnp.float32)],
        compiler_params=pltpu.CompilerParams(dimension_semantics=("arbitrary",)),
    )(index, valid, scale, channel_weights.reshape(-1), spread, innov)


def observe(state, track_row, innov_row, weight_row, footprint, channel_weights):
    tiles = to_tiles(state).astype(jnp.bfloat16)
    spread = jnp.einsum("jcab,bd->jcad", tiles, footprint, preferred_element_type=jnp.float32)
    index = jnp.clip(track_row, 0, tiles.shape[0] - 1).astype(jnp.int32)
    valid = (track_row >= 0).astype(jnp.int32)
    scale = weight_row.astype(jnp.float32)
    summed = residual_sums(spread, innov_row, index, valid, scale, channel_weights)
    forcing = jnp.einsum(
        "tcad,bd->tcab", summed, footprint.astype(jnp.float32), precision=lax.Precision.HIGHEST
    )
    return from_tiles(forcing, state.shape[1], state.shape[2])


def on_device(
    increment,
    depth_field,
    coriolis,
    footprint,
    channel_weights,
    track_tiles,
    innovations,
    obs_weights,
):
    interval = STEPS // OBS_TIMES
    rows, cols = depth_field.shape
    band = lax.axis_index("lat")
    lat_total = cols * lax.axis_size("lat")

    innov = [
        lax.all_to_all(innovations[t, 0, 0], "lon", split_axis=0, concat_axis=0, tiled=True)
        for t in range(OBS_TIMES)
    ]
    weights = obs_weights[:, 0, 0]
    weights = lax.all_to_all(weights, "lon", split_axis=1, concat_axis=1, tiled=True)
    tracks = track_tiles[:, 0, 0]

    lat_global = band * cols - HALO + jnp.arange(cols + 2 * HALO, dtype=jnp.int32)
    inside = ((lat_global >= 0) & (lat_global < lat_total))[None, :]
    cor = extend_lat(coriolis[None, :], HALO)

    fields = extend(jnp.concatenate([increment, depth_field[None]], axis=0), HALO)
    east_wind, north_wind, height, depth = fields[0], fields[1], fields[2], fields[3]
    inner = (slice(HALO, HALO + rows), slice(HALO, HALO + cols))

    def tangent_run(_, state):
        return tangent_step(*state, depth, cor, inside)

    def adjoint_run(_, state):
        return adjoint_step(*state, depth, cor, inside)

    state = (east_wind, north_wind, height)
    forcings = []
    for obs_index in range(OBS_TIMES):
        state = lax.fori_loop(0, interval, tangent_run, state)
        stacked = jnp.stack([field[inner] for field in state])
        forcing = observe(
            stacked,
            tracks[obs_index],
            innov[obs_index],
            weights[obs_index],
            footprint,
            channel_weights,
        )
        forcings.append(extend(forcing, HALO))

    state = (jnp.zeros_like(depth),) * 3
    for obs_index in range(OBS_TIMES - 1, -1, -1):
        state = tuple(field + forced for field, forced in zip(state, forcings[obs_index]))
        state = lax.fori_loop(0, interval, adjoint_run, state)
    east_adj, north_adj, height_adj = state
    adjoint = jnp.stack([east_adj[inner], north_adj[inner], height_adj[inner]])
    return increment + adjoint


def solution(mesh):
    return jax.shard_map(
        on_device,
        mesh=mesh,
        in_specs=(
            P(None, "lon", "lat"),
            P("lon", "lat"),
            P("lat"),
            P(),
            P(),
            P(None, "lat", "lon", None),
            P(None, "lat", "lon", None, None, None, None),
            P(None, "lat", "lon", None),
        ),
        out_specs=P(None, "lon", "lat"),
        check_vma=False,
    )
```

profile of v0, /device:TPU:1, one launch (start us, length us, event | category | flops | bytes accessed | tf_op | source)
XLA Modules:
  0.0 256.1 jit_solution(11831619743005337598)
XLA Ops:
  0.8 6.9 %collective-permute-start.4 = (f32[1,12]{1,0:T(1,128)S(1)}, f32[1,12]{1,0:T(1,128)S(1)}, u32[]{:S(2)}, u32[]{:S(2)}) collective-permute-start(f32[1,12]{1,0:T(1,128)S(1)} %get-tuple-element.709), channel_id=1, source_target_pairs={{0,1},{1,2},{2,3},{4,5},{5,6},{6,7},{8,9},{9,10},{10,11},{12,13},{... | collective-permute-start | bytes 152 | tf_op jit(solution)/shard_map/ppermute | solution.py:31
  7.6 1.9 collective-permute-start.5
  10.9 7.5 %all-to-all-start = ((bf16[2,32,1]{0,2,1:T(2,128)(2,1)}), bf16[2,32,1]{0,2,1:T(2,128)(2,1)S(1)}, u32[]{:S(2)}, u32[]{:S(2)}) async-start(bf16[2,32,1]{0,2,1:T(2,128)(2,1)} %copy.35), calls=%async_computation | async-start | bytes 32768 | tf_op jit(solution)/shard_map/all_to_all | solution.py:169
  23.9 4.5 %collective-permute-start.1 = (f32[4,12,256]{1,0,2:T(4,128)S(1)}, f32[4,12,256]{1,0,2:T(4,128)S(1)}, u32[]{:S(2)}, u32[]{:S(2)}) collective-permute-start(f32[4,12,256]{1,0,2:T(4,128)S(1)} %get-tuple-element.690), channel_id=1, source_target_pairs={{4,0},{8,4},{12,8},{16,12},{20,16},{24,20},{28,24},{32,28},{36,32}... | collective-permute-start | bytes 147464 | tf_op jit(solution)/shard_map/ppermute | solution.py:23
  30.2 12.8 %slice_bitcast_fusion = (bf16[32,5,128,128]{3,2,1,0:T(8,128)(2,1)}, bf16[32,5,128,128]{3,2,1,0:T(8,128)(2,1)}) fusion(bf16[2,1,1,32,5,128,128]{6,5,4,3,2,1,0:T(8,128)(2,1)} %param.22), kind=kLoop, calls=%fused_computation.66 | loop fusion | bytes 20971520 | tf_op jit(solution)/shard_map/squeeze | solution.py:165
  43.3 6.6 %collective-permute-start.2 = (f32[4,280,12]{1,0,2:T(4,128)S(1)}, f32[4,280,12]{1,0,2:T(4,128)S(1)}, u32[]{:S(2)}, u32[]{:S(2)}) collective-permute-start(f32[4,280,12]{1,0,2:T(4,128)S(1)} %get-tuple-element.683), channel_id=1, source_target_pairs={{0,1},{1,2},{2,3},{4,5},{5,6},{6,7},{8,9},{9,10},{10,11},{12,13},{... | collective-permute-start | bytes 161288 | tf_op jit(solution)/shard_map/ppermute | solution.py:31
  51.9 5.1 %all-to-all-start.2 = ((bf16[32,5,128,128]{3,2,1,0:T(8,128)(2,1)}), bf16[32,5,128,128]{3,2,1,0:T(8,128)(2,1)}, u32[]{:S(2)}, u32[]{:S(2)}) async-start(bf16[32,5,128,128]{3,2,1,0:T(8,128)(2,1)} %get-tuple-element.681), calls=%async_computation.2 | async-start | bytes 10485760 | tf_op jit(solution)/shard_map/all_to_all | solution.py:165
  58.1 2.1 pad_maximum_fusion
  64.8 4.9 %while.70 = (s32[]{:T(128)}, f32[280,280]{1,0:T(8,128)S(1)}, f32[280,280]{1,0:T(8,128)S(1)}, f32[280,280]{1,0:T(8,128)S(1)}, f32[1,280]{1,0:T(1,128)S(1)}, /*ind...) while((s32[]{:T(128)}, f32[280,280]{1,0:T(8,128)S(1)}, f32[280,280]{1,0:T(8,128)S(1)}, ...), condition=%wide.region_1.2_spmd.clone, body=%wide.region_0.1_spmd.clone.sunk | while | flops 2117922 | bytes 10980301 | solution.py:189
  70.9 45.7 %all-to-all-done.2.innov_ref = bf16[32,5,128,128]{3,2,1,0:T(8,128)(2,1)} async-done(((bf16[32,5,128,128]{3,2,1,0:T(8,128)(2,1)}), bf16[32,5,128,128]{3,2,1,0:T(8,128)(2,1)}, u32[]{:S(2)}, u32[]{:S(2)}) %all-to-all-start.2) | async-done | bytes 5242912 | tf_op jit(solution)/shard_map/all_to_all | solution.py:165
  116.6 12.5 %all-to-all-start.1 = ((bf16[32,5,128,128]{3,2,1,0:T(8,128)(2,1)}), bf16[32,5,128,128]{3,2,1,0:T(8,128)(2,1)}, u32[]{:S(2)}, u32[]{:S(2)}) async-start(bf16[32,5,128,128]{3,2,1,0:T(8,128)(2,1)} %get-tuple-element.682), calls=%async_computation.1 | async-start | bytes 10485760 | tf_op jit(solution)/shard_map/all_to_all | solution.py:165
  129.0 4.9 %while.71 = (s32[]{:T(128)}, f32[280,280]{1,0:T(8,128)S(1)}, f32[280,280]{1,0:T(8,128)S(1)}, f32[280,280]{1,0:T(8,128)S(1)}, f32[1,280]{1,0:T(1,128)S(1)}, /*ind...) while((s32[]{:T(128)}, f32[280,280]{1,0:T(8,128)S(1)}, f32[280,280]{1,0:T(8,128)S(1)}, ...), condition=%wide.region_3.4_spmd.clone, body=%wide.region_2.3_spmd.clone.sunk | while | flops 2117922 | bytes 10980301 | solution.py:189
  137.5 7.2 %shard_map.83 = f32[4,3,128,128]{3,2,1,0:T(8,128)} custom-call(s32[32]{0:T(128)} %get-tuple-element.707.index_ref, s32[32]{0:T(128)} %get-tuple-element.705.valid_ref, f32[32]{0:T(128)} %get-tuple-element.547.scale_ref, f32[15]{0:T(128)} %reshape.85.weight_ref, f32[4,3,128,128]{3,2,1,0:T(8,128)} %fusion.54.spread_ref, ...), custom_call_target="tpu_custom_call" | custom-call | tf_op jit(solution)/shard_map/pallas_call | solution.py:118
  147.5 55.6 %all-to-all-done.1.innov_ref = bf16[32,5,128,128]{3,2,1,0:T(8,128)(2,1)} async-done(((bf16[32,5,128,128]{3,2,1,0:T(8,128)(2,1)}), bf16[32,5,128,128]{3,2,1,0:T(8,128)(2,1)}, u32[]{:S(2)}, u32[]{:S(2)}) %all-to-all-start.1) | async-done | bytes 5242912 | tf_op jit(solution)/shard_map/all_to_all | solution.py:165
  203.1 7.1 %shard_map.82 = f32[4,3,128,128]{3,2,1,0:T(8,128)} custom-call(s32[32]{0:T(128)} %get-tuple-element.708.index_ref, s32[32]{0:T(128)} %get-tuple-element.706.valid_ref, f32[32]{0:T(128)} %get-tuple-element.548.scale_ref, f32[15]{0:T(128)} %reshape.85.weight_ref, f32[4,3,128,128]{3,2,1,0:T(8,128)} %fusion.58.spread_ref, ...), custom_call_target="tpu_custom_call" | custom-call | tf_op jit(solution)/shard_map/pallas_call | solution.py:118
  213.3 7.7 %collective-permute-start.7 = (f32[3,12,256]{2,1,0:T(8,128)S(1)}, f32[3,12,256]{2,1,0:T(8,128)S(1)}, u32[]{:S(2)}, u32[]{:S(2)}) collective-permute-start(f32[3,12,256]{2,1,0:T(8,128)S(1)} %get-tuple-element.704), channel_id=1, source_target_pairs={{4,0},{8,4},{12,8},{16,12},{20,16},{24,20},{28,24},{32,28},{36,32}... | collective-permute-start | bytes 110600 | tf_op jit(solution)/shard_map/ppermute | solution.py:23
  221.1 5.7 %collective-permute-start.11 = (f32[3,12,256]{2,1,0:T(8,128)S(1)}, f32[3,12,256]{2,1,0:T(8,128)S(1)}, u32[]{:S(2)}, u32[]{:S(2)}) collective-permute-start(f32[3,12,256]{2,1,0:T(8,128)S(1)} %get-tuple-element.702), channel_id=1, source_target_pairs={{4,0},{8,4},{12,8},{16,12},{20,16},{24,20},{28,24},{32,28},{36,32}... | collective-permute-start | bytes 110600 | tf_op jit(solution)/shard_map/ppermute | solution.py:23
  227.0 2.1 collective-permute-start.8
  229.1 2.9 %collective-permute-start.9 = (f32[3,280,12]{2,1,0:T(8,128)S(1)}, f32[3,280,12]{2,1,0:T(8,128)S(1)}, u32[]{:S(2)}, u32[]{:S(2)}) collective-permute-start(f32[3,280,12]{2,1,0:T(8,128)S(1)} %get-tuple-element.700), channel_id=1, source_target_pairs={{1,0},{2,1},{3,2},{5,4},{6,5},{7,6},{9,8},{10,9},{11,10},{13,12},{... | collective-permute-start | bytes 120968 | tf_op jit(solution)/shard_map/ppermute | solution.py:32
  233.2 4.1 %collective-permute-start.12 = (f32[3,280,12]{2,1,0:T(8,128)}, f32[3,280,12]{2,1,0:T(8,128)S(1)}, u32[]{:S(2)}, u32[]{:S(2)}) collective-permute-start(f32[3,280,12]{2,1,0:T(8,128)} %get-tuple-element.697), channel_id=1, source_target_pairs={{0,1},{1,2},{2,3},{4,5},{5,6},{6,7},{8,9},{9,10},{10,11},{12,13},{... | collective-permute-start | bytes 120968 | tf_op jit(solution)/shard_map/ppermute | solution.py:31
  237.3 2.2 collective-permute-start.13
  240.7 4.7 %while.72 = (s32[]{:T(128)}, f32[280,280]{1,0:T(8,128)S(1)}, f32[280,280]{1,0:T(8,128)S(1)}, f32[280,280]{1,0:T(8,128)S(1)}, f32[1,280]{1,0:T(1,128)S(1)}, /*ind...) while((s32[]{:T(128)}, f32[280,280]{1,0:T(8,128)S(1)}, f32[280,280]{1,0:T(8,128)S(1)}, ...), condition=%wide.region_5.6_spmd.clone, body=%wide.region_4.5_spmd.clone.sunk | while | flops 2196322 | bytes 10667821 | solution.py:204
  245.5 3.0 %collective-permute-done.13 = f32[3,280,12]{2,1,0:T(8,128)S(1)} collective-permute-done((f32[3,280,12]{2,1,0:T(8,128)}, f32[3,280,12]{2,1,0:T(8,128)S(1)}, u32[]{:S(2)}, u32[]{:S(2)}) %collective-permute-start.13) | collective-permute-done | bytes 40352 | tf_op jit(solution)/shard_map/ppermute | solution.py:32
  249.3 4.7 %while.73 = (s32[]{:T(128)}, f32[280,280]{1,0:T(8,128)S(1)}, f32[280,280]{1,0:T(8,128)S(1)}, f32[280,280]{1,0:T(8,128)S(1)}, f32[1,280]{1,0:T(1,128)S(1)}, /*ind...) while((s32[]{:T(128)}, f32[280,280]{1,0:T(8,128)S(1)}, f32[280,280]{1,0:T(8,128)S(1)}, ...), condition=%wide.region_7.8_spmd.clone, body=%wide.region_6.7_spmd.clone.sunk | while | flops 2196322 | bytes 10667821 | solution.py:204
  (240 shorter events, 51.6 us)
Async XLA Ops:
  0.0 135.2 %copy-start = (bf16[128,128]{1,0:T(8,128)(2,1)S(1)}, bf16[128,128]{1,0:T(8,128)(2,1)}, u32[]{:S(2)}) copy-start(bf16[128,128]{1,0:T(8,128)(2,1)} %param.19) | copy-start | bytes 98308
  0.8 42.2 %collective-permute-start.4 = (f32[1,12]{1,0:T(1,128)S(1)}, f32[1,12]{1,0:T(1,128)S(1)}, u32[]{:S(2)}, u32[]{:S(2)}) collective-permute-start(f32[1,12]{1,0:T(1,128)S(1)} %get-tuple-element.709), channel_id=1, source_target_pairs={{0,1},{1,2},{2,3},{4,5},{5,6},{6,7},{8,9},{9,10},{10,11},{12,13},{... | collective-permute-start | bytes 152 | tf_op jit(solution)/shard_map/ppermute | solution.py:31
  7.6 35.3 %collective-permute-start.5 = (f32[1,12]{1,0:T(1,128)S(1)}, f32[1,12]{1,0:T(1,128)S(1)}, u32[]{:S(2)}, u32[]{:S(2)}) collective-permute-start(f32[1,12]{1,0:T(1,128)S(1)} %get-tuple-element.710), channel_id=1, source_target_pairs={{1,0},{2,1},{3,2},{5,4},{6,5},{7,6},{9,8},{10,9},{11,10},{13,12},{... | collective-permute-start | bytes 152 | tf_op jit(solution)/shard_map/ppermute | solution.py:32
  10.9 40.9 %all-to-all-start = ((bf16[2,32,1]{0,2,1:T(2,128)(2,1)}), bf16[2,32,1]{0,2,1:T(2,128)(2,1)S(1)}, u32[]{:S(2)}, u32[]{:S(2)}) async-start(bf16[2,32,1]{0,2,1:T(2,128)(2,1)} %copy.35), calls=%async_computation | async-start | bytes 32768 | tf_op jit(solution)/shard_map/all_to_all | solution.py:169
  21.1 7.3 %copy-start.4 = (s32[2,1,1,32]{3,2,1,0:T(1,128)S(1)}, s32[2,1,1,32]{3,2,1,0:T(1,128)}, u32[]{:S(2)}) copy-start(s32[2,1,1,32]{3,2,1,0:T(1,128)} %param.21) | copy-start | bytes 772
  21.1 8.4 %copy-start.5 = (f32[5,3]{0,1:T(4,128)S(1)}, f32[5,3]{0,1:T(4,128)}, u32[]{:S(2)}) copy-start(f32[5,3]{0,1:T(4,128)} %param.20) | copy-start | bytes 184
  22.7 20.4 %collective-permute-start = (f32[4,12,256]{1,0,2:T(4,128)}, f32[4,12,256]{1,0,2:T(4,128)S(1)}, u32[]{:S(2)}, u32[]{:S(2)}) collective-permute-start(f32[4,12,256]{1,0,2:T(4,128)} %get-tuple-element.689), channel_id=1, source_target_pairs={{0,4},{4,8},{8,12},{12,16},{16,20},{20,24},{24,28},{28,32},{32,36}... | collective-permute-start | bytes 147464 | tf_op jit(solution)/shard_map/ppermute | solution.py:22
  23.9 19.2 %collective-permute-start.1 = (f32[4,12,256]{1,0,2:T(4,128)S(1)}, f32[4,12,256]{1,0,2:T(4,128)S(1)}, u32[]{:S(2)}, u32[]{:S(2)}) collective-permute-start(f32[4,12,256]{1,0,2:T(4,128)S(1)} %get-tuple-element.690), channel_id=1, source_target_pairs={{4,0},{8,4},{12,8},{16,12},{20,16},{24,20},{28,24},{32,28},{36,32}... | collective-permute-start | bytes 147464 | tf_op jit(solution)/shard_map/ppermute | solution.py:23
  30.2 12.8 %copy-start.3 = (f32[256]{0:T(256)S(1)}, f32[256]{0:T(256)}, u32[]{:S(2)}) copy-start(f32[256]{0:T(256)} %param.18) | copy-start | bytes 3076
  43.3 14.8 %collective-permute-start.2 = (f32[4,280,12]{1,0,2:T(4,128)S(1)}, f32[4,280,12]{1,0,2:T(4,128)S(1)}, u32[]{:S(2)}, u32[]{:S(2)}) collective-permute-start(f32[4,280,12]{1,0,2:T(4,128)S(1)} %get-tuple-element.683), channel_id=1, source_target_pairs={{0,1},{1,2},{2,3},{4,5},{5,6},{6,7},{8,9},{9,10},{10,11},{12,13},{... | collective-permute-start | bytes 161288 | tf_op jit(solution)/shard_map/ppermute | solution.py:31
  49.9 8.2 %collective-permute-start.3 = (f32[4,280,12]{1,0,2:T(4,128)S(1)}, f32[4,280,12]{1,0,2:T(4,128)S(1)}, u32[]{:S(2)}, u32[]{:S(2)}) collective-permute-start(f32[4,280,12]{1,0,2:T(4,128)S(1)} %get-tuple-element.684), channel_id=1, source_target_pairs={{1,0},{2,1},{3,2},{5,4},{6,5},{7,6},{9,8},{10,9},{11,10},{13,12},{... | collective-permute-start | bytes 161288 | tf_op jit(solution)/shard_map/ppermute | solution.py:32
  51.9 64.7 %all-to-all-start.2 = ((bf16[32,5,128,128]{3,2,1,0:T(8,128)(2,1)}), bf16[32,5,128,128]{3,2,1,0:T(8,128)(2,1)}, u32[]{:S(2)}, u32[]{:S(2)}) async-start(bf16[32,5,128,128]{3,2,1,0:T(8,128)(2,1)} %get-tuple-element.681), calls=%async_computation.2 | async-start | bytes 10485760 | tf_op jit(solution)/shard_map/all_to_all | solution.py:165
  116.6 86.6 %all-to-all-start.1 = ((bf16[32,5,128,128]{3,2,1,0:T(8,128)(2,1)}), bf16[32,5,128,128]{3,2,1,0:T(8,128)(2,1)}, u32[]{:S(2)}, u32[]{:S(2)}) async-start(bf16[32,5,128,128]{3,2,1,0:T(8,128)(2,1)} %get-tuple-element.682), calls=%async_computation.1 | async-start | bytes 10485760 | tf_op jit(solution)/shard_map/all_to_all | solution.py:165
  213.2 13.6 %collective-permute-start.6 = (f32[3,12,256]{2,1,0:T(8,128)S(1)}, f32[3,12,256]{2,1,0:T(8,128)S(1)}, u32[]{:S(2)}, u32[]{:S(2)}) collective-permute-start(f32[3,12,256]{2,1,0:T(8,128)S(1)} %get-tuple-element.703), channel_id=1, source_target_pairs={{0,4},{4,8},{8,12},{12,16},{16,20},{20,24},{24,28},{28,32},{32,36}... | collective-permute-start | bytes 110600 | tf_op jit(solution)/shard_map/ppermute | solution.py:22
  213.3 13.5 %collective-permute-start.7 = (f32[3,12,256]{2,1,0:T(8,128)S(1)}, f32[3,12,256]{2,1,0:T(8,128)S(1)}, u32[]{:S(2)}, u32[]{:S(2)}) collective-permute-start(f32[3,12,256]{2,1,0:T(8,128)S(1)} %get-tuple-element.704), channel_id=1, source_target_pairs={{4,0},{8,4},{12,8},{16,12},{20,16},{24,20},{28,24},{32,28},{36,32}... | collective-permute-start | bytes 110600 | tf_op jit(solution)/shard_map/ppermute | solution.py:23
  221.0 11.1 %collective-permute-start.10 = (f32[3,12,256]{2,1,0:T(8,128)S(1)}, f32[3,12,256]{2,1,0:T(8,128)S(1)}, u32[]{:S(2)}, u32[]{:S(2)}) collective-permute-start(f32[3,12,256]{2,1,0:T(8,128)S(1)} %get-tuple-element.701), channel_id=1, source_target_pairs={{0,4},{4,8},{8,12},{12,16},{16,20},{20,24},{24,28},{28,32},{32,36}... | collective-permute-start | bytes 110600 | tf_op jit(solution)/shard_map/ppermute | solution.py:22
  221.1 11.0 %collective-permute-start.11 = (f32[3,12,256]{2,1,0:T(8,128)S(1)}, f32[3,12,256]{2,1,0:T(8,128)S(1)}, u32[]{:S(2)}, u32[]{:S(2)}) collective-permute-start(f32[3,12,256]{2,1,0:T(8,128)S(1)} %get-tuple-element.702), channel_id=1, source_target_pairs={{4,0},{8,4},{12,8},{16,12},{20,16},{24,20},{28,24},{32,28},{36,32}... | collective-permute-start | bytes 110600 | tf_op jit(solution)/shard_map/ppermute | solution.py:23
  227.0 12.5 %collective-permute-start.8 = (f32[3,280,12]{2,1,0:T(8,128)S(1)}, f32[3,280,12]{2,1,0:T(8,128)S(1)}, u32[]{:S(2)}, u32[]{:S(2)}) collective-permute-start(f32[3,280,12]{2,1,0:T(8,128)S(1)} %get-tuple-element.699), channel_id=1, source_target_pairs={{0,1},{1,2},{2,3},{4,5},{5,6},{6,7},{8,9},{9,10},{10,11},{12,13},{... | collective-permute-start | bytes 120968 | tf_op jit(solution)/shard_map/ppermute | solution.py:31
  229.1 11.0 %collective-permute-start.9 = (f32[3,280,12]{2,1,0:T(8,128)S(1)}, f32[3,280,12]{2,1,0:T(8,128)S(1)}, u32[]{:S(2)}, u32[]{:S(2)}) collective-permute-start(f32[3,280,12]{2,1,0:T(8,128)S(1)} %get-tuple-element.700), channel_id=1, source_target_pairs={{1,0},{2,1},{3,2},{5,4},{6,5},{7,6},{9,8},{10,9},{11,10},{13,12},{... | collective-permute-start | bytes 120968 | tf_op jit(solution)/shard_map/ppermute | solution.py:32
  233.2 12.3 %collective-permute-start.12 = (f32[3,280,12]{2,1,0:T(8,128)}, f32[3,280,12]{2,1,0:T(8,128)S(1)}, u32[]{:S(2)}, u32[]{:S(2)}) collective-permute-start(f32[3,280,12]{2,1,0:T(8,128)} %get-tuple-element.697), channel_id=1, source_target_pairs={{0,1},{1,2},{2,3},{4,5},{5,6},{6,7},{8,9},{9,10},{10,11},{12,13},{... | collective-permute-start | bytes 120968 | tf_op jit(solution)/shard_map/ppermute | solution.py:31
  237.3 11.2 %collective-permute-start.13 = (f32[3,280,12]{2,1,0:T(8,128)}, f32[3,280,12]{2,1,0:T(8,128)S(1)}, u32[]{:S(2)}, u32[]{:S(2)}) collective-permute-start(f32[3,280,12]{2,1,0:T(8,128)} %get-tuple-element.698), channel_id=1, source_target_pairs={{1,0},{2,1},{3,2},{5,4},{6,5},{7,6},{9,8},{10,9},{11,10},{13,12},{... | collective-permute-start | bytes 120968 | tf_op jit(solution)/shard_map/ppermute | solution.py:32
  254.0 1.1 copy-start.2
  254.2 2.0 copy-start.1
where the time goes:
time: 257 us; the launch traced here: 256 us
  waiting for transfers between devices  105 us (41%)
  starting transfers between devices  72.9 us (28%)
  local copies, waits for them, and re-layouts  36.9 us (14%)
  other arithmetic  20.1 us (8%)
  Pallas kernels  14.3 us (6%)
  matrix products  5.51 us (2%)
    all_to_all x2, waiting for transfers between devices, on_device(): lax.all_to_all(innovations[t, 0, 0], 'lon', split_axis=0, concat_axis=0,...  101 us
    ppermute x4, starting transfers between devices, extend_lat(): before = lax.ppermute(x[..., length - width:], 'lat', up)  19.7 us
    ppermute x3, starting transfers between devices, extend_lon(): after = lax.ppermute(x[..., :width, :], 'lon', down)  17.8 us
    all_to_all x2, starting transfers between devices, on_device(): lax.all_to_all(innovations[t, 0, 0], 'lon', split_axis=0, concat_axis=0,...  17.6 us
    pallas_call x2, Pallas kernels, residual_sums(): pl.pallas_call(residual_kernel, grid=(owners // OWNERS_STEP,), in_specs=[...  14.3 us
    squeeze x1, local copies, waits for them, and re-layouts, on_device(): innovations[t, 0, 0]  12.8 us
    ppermute x4, starting transfers between devices, extend_lat(): after = lax.ppermute(x[..., :width], 'lat', down)  8.96 us
    all_to_all x1, starting transfers between devices, on_device(): lax.all_to_all(weights, 'lon', split_axis=1, concat_axis=1, tiled=True)  7.5 us
  transfers between devices with their start and end apart: 17, of which 4 were waited for; matrix products, arithmetic and copies ran while one was open for 20% of the time, Pallas kernels for 3%

commit v1 on v0

--- a/solution.py
+++ b/solution.py
@@ -101,7 +101,11 @@
         @pl.when(valid_ref[owner] != 0)
         def _():
             weighted = [
-                scale * (radiance_ref[j, h] - innov_ref[k, h].astype(jnp.float32))
+                scale
+                * (
+                    radiance_ref[j, h]
+                    - innov_ref[k, h * TILE : (h + 1) * TILE, :].astype(jnp.float32)
+                )
                 for h in range(channels)
             ]
             for c in range(fields):
@@ -113,7 +117,7 @@
 
 def residual_sums(spread, innov, index, valid, scale, channel_weights):
     tiles, fields = spread.shape[0], spread.shape[1]
-    owners, channels = innov.shape[0], innov.shape[1]
+    owners, channels = innov.shape[0], channel_weights.shape[0]
     smem = pl.BlockSpec(memory_space=pltpu.SMEM)
     return pl.pallas_call(
         residual_kernel,
@@ -124,7 +128,7 @@
             smem,
             smem,
             pl.BlockSpec(spread.shape, lambda s: (0, 0, 0, 0)),
-            pl.BlockSpec((OWNERS_STEP,) + innov.shape[1:], lambda s: (s, 0, 0, 0)),
+            pl.BlockSpec((OWNERS_STEP,) + innov.shape[1:], lambda s: (s, 0, 0)),
         ],
         out_specs=pl.BlockSpec(spread.shape, lambda s: (0, 0, 0, 0)),
         out_shape=jax.ShapeDtypeStruct(spread.shape, jnp.float32),
@@ -161,12 +165,17 @@
     band = lax.axis_index("lat")
     lat_total = cols * lax.axis_size("lat")
 
-    innov = [
-        lax.all_to_all(innovations[t, 0, 0], "lon", split_axis=0, concat_axis=0, tiled=True)
-        for t in range(OBS_TIMES)
-    ]
-    weights = obs_weights[:, 0, 0]
-    weights = lax.all_to_all(weights, "lon", split_axis=1, concat_axis=1, tiled=True)
+    owners, channels = innovations.shape[3], innovations.shape[4]
+    innov, weights = [], []
+    for t in range(OBS_TIMES):
+        extra = jnp.zeros((owners, 1, TILE), innovations.dtype)
+        extra = extra.at[:, 0, 0].set(obs_weights[t, 0, 0])
+        packed = jnp.concatenate(
+            [innovations[t, 0, 0].reshape(owners, channels * TILE, TILE), extra], axis=1
+        )
+        packed = lax.all_to_all(packed, "lon", split_axis=0, concat_axis=0, tiled=True)
+        innov.append(packed)
+        weights.append(packed[:, channels * TILE, 0])
     tracks = track_tiles[:, 0, 0]
 
     lat_global = band * cols - HALO + jnp.arange(cols + 2 * HALO, dtype=jnp.int32)

time: 257 us -> 251 us (0.977)
  other arithmetic: 20.1 us -> 38.8 us
  waiting for transfers between devices: 105 us -> 90.1 us
  starting transfers between devices: 72.9 us -> 60.1 us
    all_to_all x3 -> x2, waiting for transfers between devices: 101 us -> 33.6 us  [on_device(): lax.all_to_all(packed, 'lon', split_axis=0, concat_axis=0, tiled=True)]
    ppermute x3, waiting for transfers between devices: 0.01 us -> 55.4 us  [extend_lon(): after = lax.ppermute(x[..., :width, :], 'lon', down)]
    slice x0 -> x1, local copies, waits for them, and re-layouts: none -> 12.8 us  [on_device(): innovations[t, 0, 0].reshape(owners, channels * TILE, TILE)]
    squeeze x1 -> x0, local copies, waits for them, and re-layouts: 12.8 us -> none  [on_device(): innovations[t, 0, 0]]
    concatenate x0 -> x2, other arithmetic: none -> 10.5 us  [on_device(): jnp.concatenate([innovations[t, 0, 0].reshape(owners, channels * TILE, TI...]
    all_to_all x3 -> x2, starting transfers between devices: 25.1 us -> 15.8 us  [on_device(): lax.all_to_all(packed, 'lon', split_axis=0, concat_axis=0, tiled=True)]
    ppermute x3, starting transfers between devices: 17.8 us -> 12.6 us  [extend_lon(): after = lax.ppermute(x[..., :width, :], 'lon', down)]
    slice x48, local copies, waits for them, and re-layouts: 6.75 us -> 11.1 us  [lat_diff(): return 0.5 * (jnp.roll(values, -1, axis=1) - jnp.roll(values, 1, axis=1))]
  transfers between devices with their start and end apart: 17 -> 16, of which waited for: 4 -> 3; matrix products, arithmetic and copies ran while one was open for 20% -> 22% of each run, Pallas kernels for 3% -> 6%
where the time goes in v1:
time: 251 us; the launch traced here: 248 us
  waiting for transfers between devices  90.1 us (36%)
  starting transfers between devices  60.1 us (24%)
  other arithmetic  38.8 us (15%)
  local copies, waits for them, and re-layouts  38.1 us (15%)
  Pallas kernels  14.4 us (6%)
  matrix products  5.51 us (2%)
    ppermute x3, waiting for transfers between devices, extend_lon(): after = lax.ppermute(x[..., :width, :], 'lon', down)  55.4 us
    all_to_all x2, waiting for transfers between devices, on_device(): lax.all_to_all(packed, 'lon', split_axis=0, concat_axis=0, tiled=True)  33.6 us
    ppermute x4, starting transfers between devices, extend_lat(): before = lax.ppermute(x[..., length - width:], 'lat', up)  21 us
    all_to_all x2, starting transfers between devices, on_device(): lax.all_to_all(packed, 'lon', split_axis=0, concat_axis=0, tiled=True)  15.8 us
    pallas_call x2, Pallas kernels, residual_sums(): pl.pallas_call(residual_kernel, grid=(owners // OWNERS_STEP,), in_specs=[...  14.4 us
    slice x1, local copies, waits for them, and re-layouts, on_device(): innovations[t, 0, 0].reshape(owners, channels * TILE, TILE)  12.8 us
    ppermute x3, starting transfers between devices, extend_lon(): after = lax.ppermute(x[..., :width, :], 'lon', down)  12.6 us
    slice x48, local copies, waits for them, and re-layouts, lat_diff(): return 0.5 * (jnp.roll(values, -1, axis=1) - jnp.roll(values, 1, axis=1))  11.1 us
  transfers between devices with their start and end apart: 16, of which 3 were waited for; matrix products, arithmetic and copies ran while one was open for 22% of the time, Pallas kernels for 6%

profile of v1, /device:TPU:1, one launch (start us, length us, event | category | flops | bytes accessed | tf_op | source)
XLA Modules:
  0.0 248.4 jit_solution(12557965022830273970)
XLA Ops:
  0.8 12.8 %fusion.104 = (bf16[1,1,1,32,5,128,128]{6,5,4,3,2,1,0:T(8,128)(2,1)}, bf16[1,1,1,32,5,128,128]{6,5,4,3,2,1,0:T(8,128)(2,1)}) fusion(bf16[2,1,1,32,5,128,128]{6,5,4,3,2,1,0:T(8,128)(2,1)} %param.26), kind=kLoop, calls=%fused_computation.160 | loop fusion | bytes 20971520 | tf_op jit(solution)/shard_map/slice | solution.py:174
  13.7 5.2 %fusion.50 = bf16[32,641,128]{2,1,0:T(8,128)(2,1)} fusion(bf16[32,1,1]{2,1,0:T(2,128)(2,1)S(1)} %copy.26, bf16[32,640,128]{2,1,0:T(8,128)(2,1)} %bitcast.76), kind=kLoop, calls=%fused_computation.69 | loop fusion | flops 15753216 | bytes 10494016 | tf_op jit(solution)/shard_map/concatenate | solution.py:173
  18.9 9.5 %all-to-all-start = ((bf16[32,641,128]{2,1,0:T(8,128)(2,1)}), bf16[32,641,128]{2,1,0:T(8,128)(2,1)}, u32[]{:S(2)}, u32[]{:S(2)}) async-start(bf16[32,641,128]{2,1,0:T(8,128)(2,1)} %fusion.50), calls=%async_computation | async-start | bytes 10616832 | tf_op jit(solution)/shard_map/all_to_all | solution.py:176
  30.5 5.5 %collective-permute-start.1 = (f32[4,12,256]{1,0,2:T(4,128)}, f32[4,12,256]{1,0,2:T(4,128)S(1)}, u32[]{:S(2)}, u32[]{:S(2)}) collective-permute-start(f32[4,12,256]{1,0,2:T(4,128)} %get-tuple-element.684), channel_id=1, source_target_pairs={{4,0},{8,4},{12,8},{16,12},{20,16},{24,20},{28,24},{32,28},{36,32}... | collective-permute-start | bytes 147464 | tf_op jit(solution)/shard_map/ppermute | solution.py:23
  36.1 3.4 %collective-permute-start.5 = (f32[1,12]{1,0:T(1,128)S(1)}, f32[1,12]{1,0:T(1,128)S(1)}, u32[]{:S(2)}, u32[]{:S(2)}) collective-permute-start(f32[1,12]{1,0:T(1,128)S(1)} %get-tuple-element.704), channel_id=1, source_target_pairs={{1,0},{2,1},{3,2},{5,4},{6,5},{7,6},{9,8},{10,9},{11,10},{13,12},{... | collective-permute-start | bytes 152 | tf_op jit(solution)/shard_map/ppermute | solution.py:32
  39.5 5.1 %collective-permute-start.4 = (f32[1,12]{1,0:T(1,128)S(1)}, f32[1,12]{1,0:T(1,128)S(1)}, u32[]{:S(2)}, u32[]{:S(2)}) collective-permute-start(f32[1,12]{1,0:T(1,128)S(1)} %get-tuple-element.703), channel_id=1, source_target_pairs={{0,1},{1,2},{2,3},{4,5},{5,6},{6,7},{8,9},{9,10},{10,11},{12,13},{... | collective-permute-start | bytes 152 | tf_op jit(solution)/shard_map/ppermute | solution.py:31
  45.3 5.3 %fusion.51 = bf16[32,641,128]{2,1,0:T(8,128)(2,1)} fusion(bf16[32,1,1]{2,1,0:T(2,128)(2,1)S(1)} %copy.38, bf16[32,640,128]{2,1,0:T(8,128)(2,1)} %bitcast.75), kind=kLoop, calls=%fused_computation.70 | loop fusion | flops 15753216 | bytes 10494016 | tf_op jit(solution)/shard_map/concatenate | solution.py:173
  51.9 55.4 %collective-permute-done.1 = f32[4,12,256]{1,0,2:T(4,128)S(1)} collective-permute-done((f32[4,12,256]{1,0,2:T(4,128)}, f32[4,12,256]{1,0,2:T(4,128)S(1)}, u32[]{:S(2)}, u32[]{:S(2)}) %collective-permute-start.1) | collective-permute-done | bytes 49184 | tf_op jit(solution)/shard_map/ppermute | solution.py:23
  107.5 3.5 %collective-permute-start.3 = (f32[4,280,12]{1,0,2:T(4,128)S(1)}, f32[4,280,12]{1,0,2:T(4,128)S(1)}, u32[]{:S(2)}, u32[]{:S(2)}) collective-permute-start(f32[4,280,12]{1,0,2:T(4,128)S(1)} %get-tuple-element.678), channel_id=1, source_target_pairs={{1,0},{2,1},{3,2},{5,4},{6,5},{7,6},{9,8},{10,9},{11,10},{13,12},{... | collective-permute-start | bytes 161288 | tf_op jit(solution)/shard_map/ppermute | solution.py:32
  111.0 5.3 %collective-permute-start.2 = (f32[4,280,12]{1,0,2:T(4,128)S(1)}, f32[4,280,12]{1,0,2:T(4,128)S(1)}, u32[]{:S(2)}, u32[]{:S(2)}) collective-permute-start(f32[4,280,12]{1,0,2:T(4,128)S(1)} %get-tuple-element.677), channel_id=1, source_target_pairs={{0,1},{1,2},{2,3},{4,5},{5,6},{6,7},{8,9},{9,10},{10,11},{12,13},{... | collective-permute-start | bytes 161288 | tf_op jit(solution)/shard_map/ppermute | solution.py:31
  117.5 2.1 pad_maximum_fusion
  124.1 5.0 %while.72 = (s32[]{:T(128)}, f32[280,280]{1,0:T(8,128)S(1)}, f32[280,280]{1,0:T(8,128)S(1)}, f32[280,280]{1,0:T(8,128)S(1)}, f32[1,280]{1,0:T(1,128)S(1)}, /*ind...) while((s32[]{:T(128)}, f32[280,280]{1,0:T(8,128)S(1)}, f32[280,280]{1,0:T(8,128)S(1)}, ...), condition=%wide.region_1.0_spmd.clone, body=%wide.region_0.0_spmd.clone.sunk | while | flops 2117922 | bytes 10980301 | solution.py:198
  129.2 6.3 %all-to-all-start.1 = ((bf16[32,641,128]{2,1,0:T(8,128)(2,1)}), bf16[32,641,128]{2,1,0:T(8,128)(2,1)}, u32[]{:S(2)}, u32[]{:S(2)}) async-start(bf16[32,641,128]{2,1,0:T(8,128)(2,1)} %fusion.51), calls=%async_computation.1 | async-start | bytes 10616832 | tf_op jit(solution)/shard_map/all_to_all | solution.py:176
  135.6 12.6 %while.73 = (s32[]{:T(128)}, f32[280,280]{1,0:T(8,128)S(1)}, f32[280,280]{1,0:T(8,128)S(1)}, f32[280,280]{1,0:T(8,128)S(1)}, f32[1,280]{1,0:T(1,128)S(1)}, /*ind...) while((s32[]{:T(128)}, f32[280,280]{1,0:T(8,128)S(1)}, f32[280,280]{1,0:T(8,128)S(1)}, ...), condition=%wide.region_3.4_spmd.clone, body=%wide.region_2.3_spmd.clone.sunk | while | flops 2117922 | bytes 10980301 | solution.py:198
  154.5 7.3 %shard_map.82 = f32[4,3,128,128]{3,2,1,0:T(8,128)} custom-call(s32[32]{0:T(128)} %get-tuple-element.702.index_ref, s32[32]{0:T(128)} %get-tuple-element.700.valid_ref, f32[32]{0:T(128)} %fusion.65.scale_ref, f32[15]{0:T(128)} %reshape.145.weight_ref, f32[4,3,128,128]{3,2,1,0:T(8,128)} %fusion.62.spread_ref, bf16[32,641,128]{2,1,0:T(8,128)(2,1)} %all-to-all-done.innov_ref), custom_call_target="tpu_custom_call" | custom-call | tf_op jit(solution)/shard_map/pallas_call | solution.py:122
  164.7 5.3 %collective-permute-start.7 = (f32[3,12,256]{2,1,0:T(8,128)S(1)}, f32[3,12,256]{2,1,0:T(8,128)S(1)}, u32[]{:S(2)}, u32[]{:S(2)}) collective-permute-start(f32[3,12,256]{2,1,0:T(8,128)S(1)} %get-tuple-element.698), channel_id=1, source_target_pairs={{4,0},{8,4},{12,8},{16,12},{20,16},{24,20},{28,24},{32,28},{36,32}... | collective-permute-start | bytes 110600 | tf_op jit(solution)/shard_map/ppermute | solution.py:23
  170.0 33.6 %all-to-all-done.1.innov_ref = bf16[32,641,128]{2,1,0:T(8,128)(2,1)} async-done(((bf16[32,641,128]{2,1,0:T(8,128)(2,1)}), bf16[32,641,128]{2,1,0:T(8,128)(2,1)}, u32[]{:S(2)}, u32[]{:S(2)}) %all-to-all-start.1) | async-done | bytes 5251104 | tf_op jit(solution)/shard_map/all_to_all | solution.py:176
  205.3 7.1 %shard_map.83 = f32[4,3,128,128]{3,2,1,0:T(8,128)} custom-call(s32[32]{0:T(128)} %get-tuple-element.701.index_ref, s32[32]{0:T(128)} %get-tuple-element.699.valid_ref, f32[32]{0:T(128)} %fusion.64.scale_ref, f32[15]{0:T(128)} %reshape.145.weight_ref, f32[4,3,128,128]{3,2,1,0:T(8,128)} %fusion.58.spread_ref, bf16[32,641,128]{2,1,0:T(8,128)(2,1)} %all-to-all-done.1.innov_ref), custom_call_target="tpu_custom_call" | custom-call | tf_op jit(solution)/shard_map/pallas_call | solution.py:122
  220.0 5.1 %collective-permute-start.8 = (f32[3,280,12]{2,1,0:T(8,128)S(1)}, f32[3,280,12]{2,1,0:T(8,128)S(1)}, u32[]{:S(2)}, u32[]{:S(2)}) collective-permute-start(f32[3,280,12]{2,1,0:T(8,128)S(1)} %get-tuple-element.693), channel_id=1, source_target_pairs={{0,1},{1,2},{2,3},{4,5},{5,6},{6,7},{8,9},{9,10},{10,11},{12,13},{... | collective-permute-start | bytes 120968 | tf_op jit(solution)/shard_map/ppermute | solution.py:31
  228.2 5.4 %collective-permute-start.12 = (f32[3,280,12]{2,1,0:T(8,128)}, f32[3,280,12]{2,1,0:T(8,128)}, u32[]{:S(2)}, u32[]{:S(2)}) collective-permute-start(f32[3,280,12]{2,1,0:T(8,128)} %get-tuple-element.691), channel_id=1, source_target_pairs={{0,1},{1,2},{2,3},{4,5},{5,6},{6,7},{8,9},{9,10},{10,11},{12,13},{... | collective-permute-start | bytes 120968 | tf_op jit(solution)/shard_map/ppermute | solution.py:31
  234.3 4.7 %while.74 = (s32[]{:T(128)}, f32[280,280]{1,0:T(8,128)S(1)}, f32[280,280]{1,0:T(8,128)S(1)}, f32[280,280]{1,0:T(8,128)S(1)}, f32[1,280]{1,0:T(1,128)S(1)}, /*ind...) while((s32[]{:T(128)}, f32[280,280]{1,0:T(8,128)S(1)}, f32[280,280]{1,0:T(8,128)S(1)}, ...), condition=%wide.region_5.6_spmd.clone, body=%wide.region_4.5_spmd.clone.sunk | while | flops 2196322 | bytes 10667821 | solution.py:213
  239.0 1.9 pad_maximum_fusion.2
  241.1 4.8 %while.75 = (s32[]{:T(128)}, f32[280,280]{1,0:T(8,128)S(1)}, f32[280,280]{1,0:T(8,128)S(1)}, f32[280,280]{1,0:T(8,128)S(1)}, f32[1,280]{1,0:T(1,128)S(1)}, /*ind...) while((s32[]{:T(128)}, f32[280,280]{1,0:T(8,128)S(1)}, f32[280,280]{1,0:T(8,128)S(1)}, ...), condition=%wide.region_7.8_spmd.clone, body=%wide.region_6.7_spmd.clone.sunk | while | flops 2196322 | bytes 10667821 | solution.py:213
  246.3 2.1 maximum_add_fusion
  (252 shorter events, 59.8 us)
Async XLA Ops:
  0.0 150.5 %copy-start = (bf16[128,128]{1,0:T(8,128)(2,1)S(1)}, bf16[128,128]{1,0:T(8,128)(2,1)}, u32[]{:S(2)}) copy-start(bf16[128,128]{1,0:T(8,128)(2,1)} %param.23) | copy-start | bytes 98308
  18.9 9.5 %copy-start.2 = (f32[3,256,256]{2,1,0:T(8,128)S(1)}, f32[3,256,256]{2,1,0:T(8,128)}, u32[]{:S(2)}) copy-start(f32[3,256,256]{2,1,0:T(8,128)} %param.20) | copy-start | bytes 2359300
  18.9 9.9 %copy-start.3 = (f32[256,256]{1,0:T(8,128)S(1)}, f32[256,256]{1,0:T(8,128)}, u32[]{:S(2)}) copy-start(f32[256,256]{1,0:T(8,128)} %param.21) | copy-start | bytes 786436
  18.9 110.4 %all-to-all-start = ((bf16[32,641,128]{2,1,0:T(8,128)(2,1)}), bf16[32,641,128]{2,1,0:T(8,128)(2,1)}, u32[]{:S(2)}, u32[]{:S(2)}) async-start(bf16[32,641,128]{2,1,0:T(8,128)(2,1)} %fusion.50), calls=%async_computation | async-start | bytes 10616832 | tf_op jit(solution)/shard_map/all_to_all | solution.py:176
  28.3 7.7 %copy-start.6 = (f32[256]{0:T(256)S(1)}, f32[256]{0:T(256)}, u32[]{:S(2)}) copy-start(f32[256]{0:T(256)} %param.22) | copy-start | bytes 3076
  28.3 16.3 %copy-start.7 = (s32[2,1,1,32]{3,2,1,0:T(1,128)S(1)}, s32[2,1,1,32]{3,2,1,0:T(1,128)}, u32[]{:S(2)}) copy-start(s32[2,1,1,32]{3,2,1,0:T(1,128)} %param.25) | copy-start | bytes 772
  30.5 76.7 %collective-permute-start.1 = (f32[4,12,256]{1,0,2:T(4,128)}, f32[4,12,256]{1,0,2:T(4,128)S(1)}, u32[]{:S(2)}, u32[]{:S(2)}) collective-permute-start(f32[4,12,256]{1,0,2:T(4,128)} %get-tuple-element.684), channel_id=1, source_target_pairs={{4,0},{8,4},{12,8},{16,12},{20,16},{24,20},{28,24},{32,28},{36,32}... | collective-permute-start | bytes 147464 | tf_op jit(solution)/shard_map/ppermute | solution.py:23
  36.0 71.3 %collective-permute-start = (f32[4,12,256]{1,0,2:T(4,128)S(1)}, f32[4,12,256]{1,0,2:T(4,128)S(1)}, u32[]{:S(2)}, u32[]{:S(2)}) collective-permute-start(f32[4,12,256]{1,0,2:T(4,128)S(1)} %get-tuple-element.683), channel_id=1, source_target_pairs={{0,4},{4,8},{8,12},{12,16},{16,20},{20,24},{24,28},{28,32},{32,36}... | collective-permute-start | bytes 147464 | tf_op jit(solution)/shard_map/ppermute | solution.py:22
  36.1 80.2 %collective-permute-start.5 = (f32[1,12]{1,0:T(1,128)S(1)}, f32[1,12]{1,0:T(1,128)S(1)}, u32[]{:S(2)}, u32[]{:S(2)}) collective-permute-start(f32[1,12]{1,0:T(1,128)S(1)} %get-tuple-element.704), channel_id=1, source_target_pairs={{1,0},{2,1},{3,2},{5,4},{6,5},{7,6},{9,8},{10,9},{11,10},{13,12},{... | collective-permute-start | bytes 152 | tf_op jit(solution)/shard_map/ppermute | solution.py:32
  39.5 76.8 %collective-permute-start.4 = (f32[1,12]{1,0:T(1,128)S(1)}, f32[1,12]{1,0:T(1,128)S(1)}, u32[]{:S(2)}, u32[]{:S(2)}) collective-permute-start(f32[1,12]{1,0:T(1,128)S(1)} %get-tuple-element.703), channel_id=1, source_target_pairs={{0,1},{1,2},{2,3},{4,5},{5,6},{6,7},{8,9},{9,10},{10,11},{12,13},{... | collective-permute-start | bytes 152 | tf_op jit(solution)/shard_map/ppermute | solution.py:31
  45.3 5.8 %copy-start.8 = (f32[5,3]{0,1:T(4,128)S(1)}, f32[5,3]{0,1:T(4,128)}, u32[]{:S(2)}) copy-start(f32[5,3]{0,1:T(4,128)} %param.24) | copy-start | bytes 184
  107.5 8.9 %collective-permute-start.3 = (f32[4,280,12]{1,0,2:T(4,128)S(1)}, f32[4,280,12]{1,0,2:T(4,128)S(1)}, u32[]{:S(2)}, u32[]{:S(2)}) collective-permute-start(f32[4,280,12]{1,0,2:T(4,128)S(1)} %get-tuple-element.678), channel_id=1, source_target_pairs={{1,0},{2,1},{3,2},{5,4},{6,5},{7,6},{9,8},{10,9},{11,10},{13,12},{... | collective-permute-start | bytes 161288 | tf_op jit(solution)/shard_map/ppermute | solution.py:32
  111.0 6.5 %collective-permute-start.2 = (f32[4,280,12]{1,0,2:T(4,128)S(1)}, f32[4,280,12]{1,0,2:T(4,128)S(1)}, u32[]{:S(2)}, u32[]{:S(2)}) collective-permute-start(f32[4,280,12]{1,0,2:T(4,128)S(1)} %get-tuple-element.677), channel_id=1, source_target_pairs={{0,1},{1,2},{2,3},{4,5},{5,6},{6,7},{8,9},{9,10},{10,11},{12,13},{... | collective-permute-start | bytes 161288 | tf_op jit(solution)/shard_map/ppermute | solution.py:31
  129.2 74.4 %all-to-all-start.1 = ((bf16[32,641,128]{2,1,0:T(8,128)(2,1)}), bf16[32,641,128]{2,1,0:T(8,128)(2,1)}, u32[]{:S(2)}, u32[]{:S(2)}) async-start(bf16[32,641,128]{2,1,0:T(8,128)(2,1)} %fusion.51), calls=%async_computation.1 | async-start | bytes 10616832 | tf_op jit(solution)/shard_map/all_to_all | solution.py:176
  164.7 52.4 %collective-permute-start.7 = (f32[3,12,256]{2,1,0:T(8,128)S(1)}, f32[3,12,256]{2,1,0:T(8,128)S(1)}, u32[]{:S(2)}, u32[]{:S(2)}) collective-permute-start(f32[3,12,256]{2,1,0:T(8,128)S(1)} %get-tuple-element.698), channel_id=1, source_target_pairs={{4,0},{8,4},{12,8},{16,12},{20,16},{24,20},{28,24},{32,28},{36,32}... | collective-permute-start | bytes 110600 | tf_op jit(solution)/shard_map/ppermute | solution.py:23
  170.0 47.1 %collective-permute-start.6 = (f32[3,12,256]{2,1,0:T(8,128)S(1)}, f32[3,12,256]{2,1,0:T(8,128)S(1)}, u32[]{:S(2)}, u32[]{:S(2)}) collective-permute-start(f32[3,12,256]{2,1,0:T(8,128)S(1)} %get-tuple-element.697), channel_id=1, source_target_pairs={{0,4},{4,8},{8,12},{12,16},{16,20},{20,24},{24,28},{28,32},{32,36}... | collective-permute-start | bytes 110600 | tf_op jit(solution)/shard_map/ppermute | solution.py:22
  215.3 9.9 %copy-start.1 = (f32[3,256,256]{2,1,0:T(8,128)}, f32[3,256,256]{2,1,0:T(8,128)S(1)}, u32[]{:S(2)}) copy-start(f32[3,256,256]{2,1,0:T(8,128)S(1)} %reshape.150) | copy-start | bytes 2359300
  215.3 9.8 %collective-permute-start.11 = (f32[3,12,256]{2,1,0:T(8,128)S(1)}, f32[3,12,256]{2,1,0:T(8,128)S(1)}, u32[]{:S(2)}, u32[]{:S(2)}) collective-permute-start(f32[3,12,256]{2,1,0:T(8,128)S(1)} %get-tuple-element.696), channel_id=1, source_target_pairs={{4,0},{8,4},{12,8},{16,12},{20,16},{24,20},{28,24},{32,28},{36,32}... | collective-permute-start | bytes 110600 | tf_op jit(solution)/shard_map/ppermute | solution.py:23
  217.1 8.0 %collective-permute-start.10 = (f32[3,12,256]{2,1,0:T(8,128)S(1)}, f32[3,12,256]{2,1,0:T(8,128)S(1)}, u32[]{:S(2)}, u32[]{:S(2)}) collective-permute-start(f32[3,12,256]{2,1,0:T(8,128)S(1)} %get-tuple-element.695), channel_id=1, source_target_pairs={{0,4},{4,8},{8,12},{12,16},{16,20},{20,24},{24,28},{28,32},{32,36}... | collective-permute-start | bytes 110600 | tf_op jit(solution)/shard_map/ppermute | solution.py:22
  217.8 15.8 %copy-start.5 = (f32[3,12,256]{2,1,0:T(8,128)S(1)}, f32[3,12,256]{2,1,0:T(8,128)}, u32[]{:S(2)}) copy-start(f32[3,12,256]{2,1,0:T(8,128)} %copy-done.4) | copy-start | bytes 110596
  218.0 15.6 %collective-permute-start.9 = (f32[3,280,12]{2,1,0:T(8,128)S(1)}, f32[3,280,12]{2,1,0:T(8,128)S(1)}, u32[]{:S(2)}, u32[]{:S(2)}) collective-permute-start(f32[3,280,12]{2,1,0:T(8,128)S(1)} %get-tuple-element.694), channel_id=1, source_target_pairs={{1,0},{2,1},{3,2},{5,4},{6,5},{7,6},{9,8},{10,9},{11,10},{13,12},{... | collective-permute-start | bytes 120968 | tf_op jit(solution)/shard_map/ppermute | solution.py:32
  220.0 13.6 %collective-permute-start.8 = (f32[3,280,12]{2,1,0:T(8,128)S(1)}, f32[3,280,12]{2,1,0:T(8,128)S(1)}, u32[]{:S(2)}, u32[]{:S(2)}) collective-permute-start(f32[3,280,12]{2,1,0:T(8,128)S(1)} %get-tuple-element.693), channel_id=1, source_target_pairs={{0,1},{1,2},{2,3},{4,5},{5,6},{6,7},{8,9},{9,10},{10,11},{12,13},{... | collective-permute-start | bytes 120968 | tf_op jit(solution)/shard_map/ppermute | solution.py:31
  226.2 12.8 %collective-permute-start.13 = (f32[3,280,12]{2,1,0:T(8,128)}, f32[3,280,12]{2,1,0:T(8,128)}, u32[]{:S(2)}, u32[]{:S(2)}) collective-permute-start(f32[3,280,12]{2,1,0:T(8,128)} %get-tuple-element.692), channel_id=1, source_target_pairs={{1,0},{2,1},{3,2},{5,4},{6,5},{7,6},{9,8},{10,9},{11,10},{13,12},{... | collective-permute-start | bytes 120968 | tf_op jit(solution)/shard_map/ppermute | solution.py:32
  228.2 10.9 %collective-permute-start.12 = (f32[3,280,12]{2,1,0:T(8,128)}, f32[3,280,12]{2,1,0:T(8,128)}, u32[]{:S(2)}, u32[]{:S(2)}) collective-permute-start(f32[3,280,12]{2,1,0:T(8,128)} %get-tuple-element.691), channel_id=1, source_target_pairs={{0,1},{1,2},{2,3},{4,5},{5,6},{6,7},{8,9},{9,10},{10,11},{12,13},{... | collective-permute-start | bytes 120968 | tf_op jit(solution)/shard_map/ppermute | solution.py:31
  (1 other events, 0.6 us)

commit v2 on v1

--- a/solution.py
+++ b/solution.py
@@ -173,9 +173,7 @@
         packed = jnp.concatenate(
             [innovations[t, 0, 0].reshape(owners, channels * TILE, TILE), extra], axis=1
         )
-        packed = lax.all_to_all(packed, "lon", split_axis=0, concat_axis=0, tiled=True)
         innov.append(packed)
-        weights.append(packed[:, channels * TILE, 0])
     tracks = track_tiles[:, 0, 0]
 
     lat_global = band * cols - HALO + jnp.arange(cols + 2 * HALO, dtype=jnp.int32)
@@ -183,6 +181,11 @@
     cor = extend_lat(coriolis[None, :], HALO)
 
     fields = extend(jnp.concatenate([increment, depth_field[None]], axis=0), HALO)
+    fields, innov = lax.optimization_barrier((fields, innov))
+    innov = [
+        lax.all_to_all(packed, "lon", split_axis=0, concat_axis=0, tiled=True) for packed in innov
+    ]
+    weights = [packed[:, channels * TILE, 0] for packed in innov]
     east_wind, north_wind, height, depth = fields[0], fields[1], fields[2], fields[3]
     inner = (slice(HALO, HALO + rows), slice(HALO, HALO + cols))
 

time: 251 us -> 272 us (1.084)
  waiting for transfers between devices: 90.1 us -> 103 us
  local copies, waits for them, and re-layouts: 38.1 us -> 43.3 us
  other arithmetic: 38.8 us -> 41.7 us
    all_to_all x2, waiting for transfers between devices: 33.6 us -> 94 us  [on_device(): lax.all_to_all(packed, 'lon', split_axis=0, concat_axis=0, tiled=True)]
    ppermute x3, waiting for transfers between devices: 55.4 us -> 0.01 us  [extend_lon(): after = lax.ppermute(x[..., :width, :], 'lon', down)]
    ppermute x4, waiting for transfers between devices: 0.01 us -> 8.6 us  [extend_lat(): after = lax.ppermute(x[..., :width], 'lat', down)]
    ppermute x4, starting transfers between devices: 21 us -> 16.3 us  [extend_lat(): before = lax.ppermute(x[..., length - width:], 'lat', up)]
    ppermute x3, starting transfers between devices: 12.6 us -> 16.5 us  [extend_lon(): after = lax.ppermute(x[..., :width, :], 'lon', down)]
    select_n x6, other arithmetic: 5.88 us -> 9.5 us  [tangent_step(): north_next = jnp.where(inside, north_next, 0.0)]
    concatenate x2 -> x1, other arithmetic: 10.5 us -> 11.9 us  [on_device(): jnp.concatenate([innovations[t, 0, 0].reshape(owners, channels * TILE, TI...]
    unnamed x27 -> x25, local copies, waits for them, and re-layouts: 4.47 us -> 5.74 us
  transfers between devices with their start and end apart: 16 -> 16, of which waited for: 3 -> 5; matrix products, arithmetic and copies ran while one was open for 22% -> 25% of each run, Pallas kernels for 6% -> 3%
where the time goes in v2:
time: 272 us; the launch traced here: 270 us
  waiting for transfers between devices  103 us (38%)
  starting transfers between devices  61.8 us (23%)
  local copies, waits for them, and re-layouts  43.3 us (16%)
  other arithmetic  41.7 us (15%)
  Pallas kernels  14.2 us (5%)
  matrix products  5.49 us (2%)
    all_to_all x2, waiting for transfers between devices, on_device(): lax.all_to_all(packed, 'lon', split_axis=0, concat_axis=0, tiled=True)  94 us
    all_to_all x2, starting transfers between devices, on_device(): lax.all_to_all(packed, 'lon', split_axis=0, concat_axis=0, tiled=True)  16.7 us
    ppermute x3, starting transfers between devices, extend_lon(): after = lax.ppermute(x[..., :width, :], 'lon', down)  16.5 us
    ppermute x4, starting transfers between devices, extend_lat(): before = lax.ppermute(x[..., length - width:], 'lat', up)  16.3 us
    pallas_call x2, Pallas kernels, residual_sums(): pl.pallas_call(residual_kernel, grid=(owners // OWNERS_STEP,), in_specs=[...  14.2 us
    slice x48, local copies, waits for them, and re-layouts, lat_diff(): return 0.5 * (jnp.roll(values, -1, axis=1) - jnp.roll(values, 1, axis=1))  13 us
    slice x1, local copies, waits for them, and re-layouts, on_device(): innovations[t, 0, 0].reshape(owners, channels * TILE, TILE)  12.8 us
    concatenate x1, other arithmetic, on_device(): jnp.concatenate([innovations[t, 0, 0].reshape(owners, channels * TILE, TI...  11.9 us
  transfers between devices with their start and end apart: 16, of which 5 were waited for; matrix products, arithmetic and copies ran while one was open for 25% of the time, Pallas kernels for 3%

profile of v2, /device:TPU:1, one launch (start us, length us, event | category | flops | bytes accessed | tf_op | source)
XLA Modules:
  0.0 270.4 jit_solution(10053961234925318615)
XLA Ops:
  2.5 2.1 collective-permute-start
  4.6 5.2 %collective-permute-start.1 = (f32[4,12,256]{1,0,2:T(4,128)S(1)}, f32[4,12,256]{1,0,2:T(4,128)S(1)}, u32[]{:S(2)}, u32[]{:S(2)}) collective-permute-start(f32[4,12,256]{1,0,2:T(4,128)S(1)} %get-tuple-element.690), channel_id=1, source_target_pairs={{4,0},{8,4},{12,8},{16,12},{20,16},{24,20},{28,24},{32,28},{36,32}... | collective-permute-start | bytes 147464 | tf_op jit(solution)/shard_map/ppermute | solution.py:23
  9.9 6.0 %collective-permute-start.4 = (f32[1,12]{1,0:T(1,128)S(1)}, f32[1,12]{1,0:T(1,128)S(1)}, u32[]{:S(2)}, u32[]{:S(2)}) collective-permute-start(f32[1,12]{1,0:T(1,128)S(1)} %get-tuple-element.709), channel_id=1, source_target_pairs={{0,1},{1,2},{2,3},{4,5},{5,6},{6,7},{8,9},{9,10},{10,11},{12,13},{... | collective-permute-start | bytes 152 | tf_op jit(solution)/shard_map/ppermute | solution.py:31
  17.9 12.8 %fusion.104 = (bf16[1,1,1,32,5,128,128]{6,5,4,3,2,1,0:T(8,128)(2,1)}, bf16[1,1,1,32,5,128,128]{6,5,4,3,2,1,0:T(8,128)(2,1)}) fusion(bf16[2,1,1,32,5,128,128]{6,5,4,3,2,1,0:T(8,128)(2,1)} %param.26), kind=kLoop, calls=%fused_computation.160 | loop fusion | bytes 20971520 | tf_op jit(solution)/shard_map/slice | solution.py:174
  31.5 11.9 %fusion.50 = (bf16[32,641,128]{2,1,0:T(8,128)(2,1)}, bf16[32,641,128]{2,1,0:T(8,128)(2,1)}) fusion(bf16[32,1,1]{2,1,0:T(2,128)(2,1)S(1)} %copy.28, bf16[32,640,128]{2,1,0:T(8,128)(2,1)} %bitcast.76, bf16[32,1,1]{2,1,0:T(2,128)(2,1)S(1)} %copy.29, bf16[32,640,128]{2,1,0:T(8,128)(2,1)} %bitcast.75), kind=kLoop, calls=%fused_computation.69 | loop fusion | flops 28880896 | bytes 20988032 | tf_op jit(solution)/shard_map/concatenate | solution.py:173
  45.0 5.1 %collective-permute-start.2 = (f32[4,280,12]{1,0,2:T(4,128)S(1)}, f32[4,280,12]{1,0,2:T(4,128)S(1)}, u32[]{:S(2)}, u32[]{:S(2)}) collective-permute-start(f32[4,280,12]{1,0,2:T(4,128)S(1)} %get-tuple-element.683), channel_id=1, source_target_pairs={{0,1},{1,2},{2,3},{4,5},{5,6},{6,7},{8,9},{9,10},{10,11},{12,13},{... | collective-permute-start | bytes 161288 | tf_op jit(solution)/shard_map/ppermute | solution.py:31
  50.1 2.1 collective-permute-start.3
  52.3 5.0 %collective-permute-done.3 = f32[4,280,12]{1,0,2:T(4,128)S(1)} collective-permute-done((f32[4,280,12]{1,0,2:T(4,128)S(1)}, f32[4,280,12]{1,0,2:T(4,128)S(1)}, u32[]{:S(2)}, u32[]{:S(2)}) %collective-permute-start.3) | collective-permute-done | bytes 53792 | tf_op jit(solution)/shard_map/ppermute | solution.py:32
  63.9 4.9 %all-to-all-start.1 = ((bf16[32,641,128]{2,1,0:T(8,128)(2,1)}), bf16[32,641,128]{2,1,0:T(8,128)(2,1)}, u32[]{:S(2)}, u32[]{:S(2)}) async-start(bf16[32,641,128]{2,1,0:T(8,128)(2,1)} %get-tuple-element.447), calls=%async_computation.1 | async-start | bytes 10616832 | tf_op jit(solution)/shard_map/all_to_all | solution.py:186
  68.8 9.8 %while.72 = (s32[]{:T(128)}, f32[280,280]{1,0:T(8,128)S(1)}, f32[280,280]{1,0:T(8,128)S(1)}, f32[280,280]{1,0:T(8,128)S(1)}, f32[1,280]{1,0:T(1,128)S(1)}, /*ind...) while((s32[]{:T(128)}, f32[280,280]{1,0:T(8,128)S(1)}, f32[280,280]{1,0:T(8,128)S(1)}, ...), condition=%wide.region_1.0_spmd.clone, body=%wide.region_0.0_spmd.clone.sunk | while | flops 2117922 | bytes 10980301 | solution.py:201
  78.7 50.7 %all-to-all-done.1.innov_ref = bf16[32,641,128]{2,1,0:T(8,128)(2,1)} async-done(((bf16[32,641,128]{2,1,0:T(8,128)(2,1)}), bf16[32,641,128]{2,1,0:T(8,128)(2,1)}, u32[]{:S(2)}, u32[]{:S(2)}) %all-to-all-start.1) | async-done | bytes 5251104 | tf_op jit(solution)/shard_map/all_to_all | solution.py:186
  129.5 11.8 %all-to-all-start = ((bf16[32,641,128]{2,1,0:T(8,128)(2,1)}), bf16[32,641,128]{2,1,0:T(8,128)(2,1)}, u32[]{:S(2)}, u32[]{:S(2)}) async-start(bf16[32,641,128]{2,1,0:T(8,128)(2,1)} %get-tuple-element.438), calls=%async_computation | async-start | bytes 10616832 | tf_op jit(solution)/shard_map/all_to_all | solution.py:186
  141.2 15.9 %while.73 = (s32[]{:T(128)}, f32[280,280]{1,0:T(8,128)S(1)}, f32[280,280]{1,0:T(8,128)S(1)}, f32[280,280]{1,0:T(8,128)S(1)}, f32[1,280]{1,0:T(1,128)S(1)}, /*ind...) while((s32[]{:T(128)}, f32[280,280]{1,0:T(8,128)S(1)}, f32[280,280]{1,0:T(8,128)S(1)}, ...), condition=%wide.region_3.4_spmd.clone, body=%wide.region_2.3_spmd.clone.sunk | while | flops 2117922 | bytes 10980301 | solution.py:201
  163.6 6.9 %shard_map.83 = f32[4,3,128,128]{3,2,1,0:T(8,128)} custom-call(s32[32]{0:T(128)} %get-tuple-element.707.index_ref, s32[32]{0:T(128)} %get-tuple-element.705.valid_ref, f32[32]{0:T(128)} %fusion.64.scale_ref, f32[15]{0:T(128)} %reshape.146.weight_ref, f32[4,3,128,128]{3,2,1,0:T(8,128)} %fusion.58.spread_ref, bf16[32,641,128]{2,1,0:T(8,128)(2,1)} %all-to-all-done.1.innov_ref), custom_call_target="tpu_custom_call" | custom-call | tf_op jit(solution)/shard_map/pallas_call | solution.py:122
  173.3 43.3 %all-to-all-done.innov_ref = bf16[32,641,128]{2,1,0:T(8,128)(2,1)} async-done(((bf16[32,641,128]{2,1,0:T(8,128)(2,1)}), bf16[32,641,128]{2,1,0:T(8,128)(2,1)}, u32[]{:S(2)}, u32[]{:S(2)}) %all-to-all-start) | async-done | bytes 5251104 | tf_op jit(solution)/shard_map/all_to_all | solution.py:186
  218.4 7.3 %shard_map.82 = f32[4,3,128,128]{3,2,1,0:T(8,128)} custom-call(s32[32]{0:T(128)} %get-tuple-element.708.index_ref, s32[32]{0:T(128)} %get-tuple-element.706.valid_ref, f32[32]{0:T(128)} %fusion.65.scale_ref, f32[15]{0:T(128)} %reshape.146.weight_ref, f32[4,3,128,128]{3,2,1,0:T(8,128)} %fusion.62.spread_ref, bf16[32,641,128]{2,1,0:T(8,128)(2,1)} %all-to-all-done.innov_ref), custom_call_target="tpu_custom_call" | custom-call | tf_op jit(solution)/shard_map/pallas_call | solution.py:122
  228.6 5.7 %collective-permute-start.7 = (f32[3,12,256]{2,1,0:T(8,128)S(1)}, f32[3,12,256]{2,1,0:T(8,128)S(1)}, u32[]{:S(2)}, u32[]{:S(2)}) collective-permute-start(f32[3,12,256]{2,1,0:T(8,128)S(1)} %get-tuple-element.704), channel_id=1, source_target_pairs={{4,0},{8,4},{12,8},{16,12},{20,16},{24,20},{28,24},{32,28},{36,32}... | collective-permute-start | bytes 110600 | tf_op jit(solution)/shard_map/ppermute | solution.py:23
  234.4 5.7 %collective-permute-start.11 = (f32[3,12,256]{2,1,0:T(8,128)S(1)}, f32[3,12,256]{2,1,0:T(8,128)S(1)}, u32[]{:S(2)}, u32[]{:S(2)}) collective-permute-start(f32[3,12,256]{2,1,0:T(8,128)S(1)} %get-tuple-element.702), channel_id=1, source_target_pairs={{4,0},{8,4},{12,8},{16,12},{20,16},{24,20},{28,24},{32,28},{36,32}... | collective-permute-start | bytes 110600 | tf_op jit(solution)/shard_map/ppermute | solution.py:23
  242.2 3.9 %collective-permute-start.9 = (f32[3,280,12]{2,1,0:T(8,128)S(1)}, f32[3,280,12]{2,1,0:T(8,128)S(1)}, u32[]{:S(2)}, u32[]{:S(2)}) collective-permute-start(f32[3,280,12]{2,1,0:T(8,128)S(1)} %get-tuple-element.700), channel_id=1, source_target_pairs={{1,0},{2,1},{3,2},{5,4},{6,5},{7,6},{9,8},{10,9},{11,10},{13,12},{... | collective-permute-start | bytes 120968 | tf_op jit(solution)/shard_map/ppermute | solution.py:32
  247.2 3.2 %collective-permute-start.12 = (f32[3,280,12]{2,1,0:T(8,128)}, f32[3,280,12]{2,1,0:T(8,128)S(1)}, u32[]{:S(2)}, u32[]{:S(2)}) collective-permute-start(f32[3,280,12]{2,1,0:T(8,128)} %get-tuple-element.697), channel_id=1, source_target_pairs={{0,1},{1,2},{2,3},{4,5},{5,6},{6,7},{8,9},{9,10},{10,11},{12,13},{... | collective-permute-start | bytes 120968 | tf_op jit(solution)/shard_map/ppermute | solution.py:31
  250.4 2.2 collective-permute-start.13
  253.9 4.8 %while.74 = (s32[]{:T(128)}, f32[280,280]{1,0:T(8,128)S(1)}, f32[280,280]{1,0:T(8,128)S(1)}, f32[280,280]{1,0:T(8,128)S(1)}, f32[1,280]{1,0:T(1,128)S(1)}, /*ind...) while((s32[]{:T(128)}, f32[280,280]{1,0:T(8,128)S(1)}, f32[280,280]{1,0:T(8,128)S(1)}, ...), condition=%wide.region_5.6_spmd.clone, body=%wide.region_4.5_spmd.clone.sunk | while | flops 2196322 | bytes 10667821 | solution.py:216
  258.7 3.0 %collective-permute-done.13 = f32[3,280,12]{2,1,0:T(8,128)} collective-permute-done((f32[3,280,12]{2,1,0:T(8,128)}, f32[3,280,12]{2,1,0:T(8,128)}, u32[]{:S(2)}, u32[]{:S(2)}) %collective-permute-start.13) | collective-permute-done | bytes 40352 | tf_op jit(solution)/shard_map/ppermute | solution.py:32
  263.5 4.8 %while.75 = (s32[]{:T(128)}, f32[280,280]{1,0:T(8,128)S(1)}, f32[280,280]{1,0:T(8,128)S(1)}, f32[280,280]{1,0:T(8,128)S(1)}, f32[1,280]{1,0:T(1,128)S(1)}, /*ind...) while((s32[]{:T(128)}, f32[280,280]{1,0:T(8,128)S(1)}, f32[280,280]{1,0:T(8,128)S(1)}, ...), condition=%wide.region_7.8_spmd.clone, body=%wide.region_6.7_spmd.clone.sunk | while | flops 2196322 | bytes 10667821 | solution.py:216
  (250 shorter events, 70.5 us)
Async XLA Ops:
  0.0 159.5 %copy-start = (bf16[128,128]{1,0:T(8,128)(2,1)S(1)}, bf16[128,128]{1,0:T(8,128)(2,1)}, u32[]{:S(2)}) copy-start(bf16[128,128]{1,0:T(8,128)(2,1)} %param.23) | copy-start | bytes 98308
  0.0 1.6 copy-start.3
  1.6 8.2 %copy-start.4 = (f32[256]{0:T(256)S(1)}, f32[256]{0:T(256)}, u32[]{:S(2)}) copy-start(f32[256]{0:T(256)} %param.22) | copy-start | bytes 3076
  2.5 42.2 %collective-permute-start = (f32[4,12,256]{1,0,2:T(4,128)S(1)}, f32[4,12,256]{1,0,2:T(4,128)S(1)}, u32[]{:S(2)}, u32[]{:S(2)}) collective-permute-start(f32[4,12,256]{1,0,2:T(4,128)S(1)} %get-tuple-element.689), channel_id=1, source_target_pairs={{0,4},{4,8},{8,12},{12,16},{16,20},{20,24},{24,28},{28,32},{32,36}... | collective-permute-start | bytes 147464 | tf_op jit(solution)/shard_map/ppermute | solution.py:22
  4.6 40.1 %collective-permute-start.1 = (f32[4,12,256]{1,0,2:T(4,128)S(1)}, f32[4,12,256]{1,0,2:T(4,128)S(1)}, u32[]{:S(2)}, u32[]{:S(2)}) collective-permute-start(f32[4,12,256]{1,0,2:T(4,128)S(1)} %get-tuple-element.690), channel_id=1, source_target_pairs={{4,0},{8,4},{12,8},{16,12},{20,16},{24,20},{28,24},{32,28},{36,32}... | collective-permute-start | bytes 147464 | tf_op jit(solution)/shard_map/ppermute | solution.py:23
  9.9 42.4 %collective-permute-start.4 = (f32[1,12]{1,0:T(1,128)S(1)}, f32[1,12]{1,0:T(1,128)S(1)}, u32[]{:S(2)}, u32[]{:S(2)}) collective-permute-start(f32[1,12]{1,0:T(1,128)S(1)} %get-tuple-element.709), channel_id=1, source_target_pairs={{0,1},{1,2},{2,3},{4,5},{5,6},{6,7},{8,9},{9,10},{10,11},{12,13},{... | collective-permute-start | bytes 152 | tf_op jit(solution)/shard_map/ppermute | solution.py:31
  15.9 14.8 %copy-start.7 = (bf16[2,1,1,32]{3,0,2,1:T(2,128)(2,1)S(1)}, bf16[2,1,1,32]{3,0,2,1:T(2,128)(2,1)}, u32[]{:S(2)}) copy-start(bf16[2,1,1,32]{3,0,2,1:T(2,128)(2,1)} %param.27) | copy-start | bytes 388
  15.9 15.0 %copy-start.5 = (s32[2,1,1,32]{3,2,1,0:T(1,128)S(1)}, s32[2,1,1,32]{3,2,1,0:T(1,128)}, u32[]{:S(2)}) copy-start(s32[2,1,1,32]{3,2,1,0:T(1,128)} %param.25) | copy-start | bytes 772
  15.9 36.3 %collective-permute-start.5 = (f32[1,12]{1,0:T(1,128)S(1)}, f32[1,12]{1,0:T(1,128)S(1)}, u32[]{:S(2)}, u32[]{:S(2)}) collective-permute-start(f32[1,12]{1,0:T(1,128)S(1)} %get-tuple-element.710), channel_id=1, source_target_pairs={{1,0},{2,1},{3,2},{5,4},{6,5},{7,6},{9,8},{10,9},{11,10},{13,12},{... | collective-permute-start | bytes 152 | tf_op jit(solution)/shard_map/ppermute | solution.py:32
  31.5 12.4 %copy-start.6 = (f32[5,3]{0,1:T(4,128)S(1)}, f32[5,3]{0,1:T(4,128)}, u32[]{:S(2)}) copy-start(f32[5,3]{0,1:T(4,128)} %param.24) | copy-start | bytes 184
  45.0 7.4 %collective-permute-start.2 = (f32[4,280,12]{1,0,2:T(4,128)S(1)}, f32[4,280,12]{1,0,2:T(4,128)S(1)}, u32[]{:S(2)}, u32[]{:S(2)}) collective-permute-start(f32[4,280,12]{1,0,2:T(4,128)S(1)} %get-tuple-element.683), channel_id=1, source_target_pairs={{0,1},{1,2},{2,3},{4,5},{5,6},{6,7},{8,9},{9,10},{10,11},{12,13},{... | collective-permute-start | bytes 161288 | tf_op jit(solution)/shard_map/ppermute | solution.py:31
  50.1 7.2 %collective-permute-start.3 = (f32[4,280,12]{1,0,2:T(4,128)S(1)}, f32[4,280,12]{1,0,2:T(4,128)S(1)}, u32[]{:S(2)}, u32[]{:S(2)}) collective-permute-start(f32[4,280,12]{1,0,2:T(4,128)S(1)} %get-tuple-element.684), channel_id=1, source_target_pairs={{1,0},{2,1},{3,2},{5,4},{6,5},{7,6},{9,8},{10,9},{11,10},{13,12},{... | collective-permute-start | bytes 161288 | tf_op jit(solution)/shard_map/ppermute | solution.py:32
  63.9 65.5 %all-to-all-start.1 = ((bf16[32,641,128]{2,1,0:T(8,128)(2,1)}), bf16[32,641,128]{2,1,0:T(8,128)(2,1)}, u32[]{:S(2)}, u32[]{:S(2)}) async-start(bf16[32,641,128]{2,1,0:T(8,128)(2,1)} %get-tuple-element.447), calls=%async_computation.1 | async-start | bytes 10616832 | tf_op jit(solution)/shard_map/all_to_all | solution.py:186
  129.5 87.2 %all-to-all-start = ((bf16[32,641,128]{2,1,0:T(8,128)(2,1)}), bf16[32,641,128]{2,1,0:T(8,128)(2,1)}, u32[]{:S(2)}, u32[]{:S(2)}) async-start(bf16[32,641,128]{2,1,0:T(8,128)(2,1)} %get-tuple-element.438), calls=%async_computation | async-start | bytes 10616832 | tf_op jit(solution)/shard_map/all_to_all | solution.py:186
  228.5 11.5 %collective-permute-start.6 = (f32[3,12,256]{2,1,0:T(8,128)S(1)}, f32[3,12,256]{2,1,0:T(8,128)S(1)}, u32[]{:S(2)}, u32[]{:S(2)}) collective-permute-start(f32[3,12,256]{2,1,0:T(8,128)S(1)} %get-tuple-element.703), channel_id=1, source_target_pairs={{0,4},{4,8},{8,12},{12,16},{16,20},{20,24},{24,28},{28,32},{32,36}... | collective-permute-start | bytes 110600 | tf_op jit(solution)/shard_map/ppermute | solution.py:22
  228.6 11.4 %collective-permute-start.7 = (f32[3,12,256]{2,1,0:T(8,128)S(1)}, f32[3,12,256]{2,1,0:T(8,128)S(1)}, u32[]{:S(2)}, u32[]{:S(2)}) collective-permute-start(f32[3,12,256]{2,1,0:T(8,128)S(1)} %get-tuple-element.704), channel_id=1, source_target_pairs={{4,0},{8,4},{12,8},{16,12},{20,16},{24,20},{28,24},{32,28},{36,32}... | collective-permute-start | bytes 110600 | tf_op jit(solution)/shard_map/ppermute | solution.py:23
  234.3 11.8 %collective-permute-start.10 = (f32[3,12,256]{2,1,0:T(8,128)S(1)}, f32[3,12,256]{2,1,0:T(8,128)S(1)}, u32[]{:S(2)}, u32[]{:S(2)}) collective-permute-start(f32[3,12,256]{2,1,0:T(8,128)S(1)} %get-tuple-element.701), channel_id=1, source_target_pairs={{0,4},{4,8},{8,12},{12,16},{16,20},{20,24},{24,28},{28,32},{32,36}... | collective-permute-start | bytes 110600 | tf_op jit(solution)/shard_map/ppermute | solution.py:22
  234.4 11.7 %collective-permute-start.11 = (f32[3,12,256]{2,1,0:T(8,128)S(1)}, f32[3,12,256]{2,1,0:T(8,128)S(1)}, u32[]{:S(2)}, u32[]{:S(2)}) collective-permute-start(f32[3,12,256]{2,1,0:T(8,128)S(1)} %get-tuple-element.702), channel_id=1, source_target_pairs={{4,0},{8,4},{12,8},{16,12},{20,16},{24,20},{28,24},{32,28},{36,32}... | collective-permute-start | bytes 110600 | tf_op jit(solution)/shard_map/ppermute | solution.py:23
  240.3 12.3 %collective-permute-start.8 = (f32[3,280,12]{2,1,0:T(8,128)S(1)}, f32[3,280,12]{2,1,0:T(8,128)S(1)}, u32[]{:S(2)}, u32[]{:S(2)}) collective-permute-start(f32[3,280,12]{2,1,0:T(8,128)S(1)} %get-tuple-element.699), channel_id=1, source_target_pairs={{0,1},{1,2},{2,3},{4,5},{5,6},{6,7},{8,9},{9,10},{10,11},{12,13},{... | collective-permute-start | bytes 120968 | tf_op jit(solution)/shard_map/ppermute | solution.py:31
  242.2 11.0 %collective-permute-start.9 = (f32[3,280,12]{2,1,0:T(8,128)S(1)}, f32[3,280,12]{2,1,0:T(8,128)S(1)}, u32[]{:S(2)}, u32[]{:S(2)}) collective-permute-start(f32[3,280,12]{2,1,0:T(8,128)S(1)} %get-tuple-element.700), channel_id=1, source_target_pairs={{1,0},{2,1},{3,2},{5,4},{6,5},{7,6},{9,8},{10,9},{11,10},{13,12},{... | collective-permute-start | bytes 120968 | tf_op jit(solution)/shard_map/ppermute | solution.py:32
  247.2 11.5 %collective-permute-start.12 = (f32[3,280,12]{2,1,0:T(8,128)}, f32[3,280,12]{2,1,0:T(8,128)S(1)}, u32[]{:S(2)}, u32[]{:S(2)}) collective-permute-start(f32[3,280,12]{2,1,0:T(8,128)} %get-tuple-element.697), channel_id=1, source_target_pairs={{0,1},{1,2},{2,3},{4,5},{5,6},{6,7},{8,9},{9,10},{10,11},{12,13},{... | collective-permute-start | bytes 120968 | tf_op jit(solution)/shard_map/ppermute | solution.py:31
  250.4 11.3 %collective-permute-start.13 = (f32[3,280,12]{2,1,0:T(8,128)}, f32[3,280,12]{2,1,0:T(8,128)}, u32[]{:S(2)}, u32[]{:S(2)}) collective-permute-start(f32[3,280,12]{2,1,0:T(8,128)} %get-tuple-element.698), channel_id=1, source_target_pairs={{1,0},{2,1},{3,2},{5,4},{6,5},{7,6},{9,8},{10,9},{11,10},{13,12},{... | collective-permute-start | bytes 120968 | tf_op jit(solution)/shard_map/ppermute | solution.py:32
  268.3 1.1 copy-start.2
  268.3 2.1 copy-start.1

commit v3 on v1

--- a/solution.py
+++ b/solution.py
@@ -9,7 +9,7 @@
 STEPS = 6
 OBS_TIMES = 2
 HALO = 2 * STEPS
-OWNERS_STEP = 4
+OWNERS_STEP = 8
 
 
 COURANT = 0.7

time: 251 us -> 249 us (level)
  Pallas kernels: 14.4 us -> 10.7 us
    pallas_call x2, Pallas kernels: 14.4 us -> 10.7 us  [residual_sums(): pl.pallas_call(residual_kernel, grid=(owners // OWNERS_STEP,), in_specs=[...]
  transfers between devices with their start and end apart: 16 -> 16, of which waited for: 3 -> 3; matrix products, arithmetic and copies ran while one was open for 22% -> 22% of each run, Pallas kernels for 6% -> 4%
where the time goes in v3:
time: 249 us; the launch traced here: 247 us
  waiting for transfers between devices  91.5 us (37%)
  starting transfers between devices  60.6 us (24%)
  other arithmetic  38.8 us (16%)
  local copies, waits for them, and re-layouts  38.1 us (15%)
  Pallas kernels  10.7 us (4%)
  matrix products  5.51 us (2%)
    ppermute x3, waiting for transfers between devices, extend_lon(): after = lax.ppermute(x[..., :width, :], 'lon', down)  55.4 us
    all_to_all x2, waiting for transfers between devices, on_device(): lax.all_to_all(packed, 'lon', split_axis=0, concat_axis=0, tiled=True)  35 us
    ppermute x4, starting transfers between devices, extend_lat(): before = lax.ppermute(x[..., length - width:], 'lat', up)  20.7 us
    all_to_all x2, starting transfers between devices, on_device(): lax.all_to_all(packed, 'lon', split_axis=0, concat_axis=0, tiled=True)  15.8 us
    ppermute x3, starting transfers between devices, extend_lon(): after = lax.ppermute(x[..., :width, :], 'lon', down)  13.4 us
    slice x1, local copies, waits for them, and re-layouts, on_device(): innovations[t, 0, 0].reshape(owners, channels * TILE, TILE)  12.8 us
    slice x48, local copies, waits for them, and re-layouts, lat_diff(): return 0.5 * (jnp.roll(values, -1, axis=1) - jnp.roll(values, 1, axis=1))  11.1 us
    ppermute x4, starting transfers between devices, extend_lat(): after = lax.ppermute(x[..., :width], 'lat', down)  10.7 us
  transfers between devices with their start and end apart: 16, of which 3 were waited for; matrix products, arithmetic and copies ran while one was open for 22% of the time, Pallas kernels for 4%

profile of v3, /device:TPU:1, one launch (start us, length us, event | category | flops | bytes accessed | tf_op | source)
XLA Modules:
  0.0 246.6 jit_solution(8041418194481837784)
XLA Ops:
  0.8 12.8 %fusion.104 = (bf16[1,1,1,32,5,128,128]{6,5,4,3,2,1,0:T(8,128)(2,1)}, bf16[1,1,1,32,5,128,128]{6,5,4,3,2,1,0:T(8,128)(2,1)}) fusion(bf16[2,1,1,32,5,128,128]{6,5,4,3,2,1,0:T(8,128)(2,1)} %param.26), kind=kLoop, calls=%fused_computation.160 | loop fusion | bytes 20971520 | tf_op jit(solution)/shard_map/slice | solution.py:174
  13.7 5.2 %fusion.50 = bf16[32,641,128]{2,1,0:T(8,128)(2,1)} fusion(bf16[32,1,1]{2,1,0:T(2,128)(2,1)S(1)} %copy.26, bf16[32,640,128]{2,1,0:T(8,128)(2,1)} %bitcast.76), kind=kLoop, calls=%fused_computation.69 | loop fusion | flops 15753216 | bytes 10494016 | tf_op jit(solution)/shard_map/concatenate | solution.py:173
  18.9 9.5 %all-to-all-start = ((bf16[32,641,128]{2,1,0:T(8,128)(2,1)}), bf16[32,641,128]{2,1,0:T(8,128)(2,1)}, u32[]{:S(2)}, u32[]{:S(2)}) async-start(bf16[32,641,128]{2,1,0:T(8,128)(2,1)} %fusion.50), calls=%async_computation | async-start | bytes 10616832 | tf_op jit(solution)/shard_map/all_to_all | solution.py:176
  30.5 5.5 %collective-permute-start.1 = (f32[4,12,256]{1,0,2:T(4,128)}, f32[4,12,256]{1,0,2:T(4,128)S(1)}, u32[]{:S(2)}, u32[]{:S(2)}) collective-permute-start(f32[4,12,256]{1,0,2:T(4,128)} %get-tuple-element.684), channel_id=1, source_target_pairs={{4,0},{8,4},{12,8},{16,12},{20,16},{24,20},{28,24},{32,28},{36,32}... | collective-permute-start | bytes 147464 | tf_op jit(solution)/shard_map/ppermute | solution.py:23
  36.1 3.4 %collective-permute-start.5 = (f32[1,12]{1,0:T(1,128)S(1)}, f32[1,12]{1,0:T(1,128)S(1)}, u32[]{:S(2)}, u32[]{:S(2)}) collective-permute-start(f32[1,12]{1,0:T(1,128)S(1)} %get-tuple-element.704), channel_id=1, source_target_pairs={{1,0},{2,1},{3,2},{5,4},{6,5},{7,6},{9,8},{10,9},{11,10},{13,12},{... | collective-permute-start | bytes 152 | tf_op jit(solution)/shard_map/ppermute | solution.py:32
  39.5 5.1 %collective-permute-start.4 = (f32[1,12]{1,0:T(1,128)S(1)}, f32[1,12]{1,0:T(1,128)S(1)}, u32[]{:S(2)}, u32[]{:S(2)}) collective-permute-start(f32[1,12]{1,0:T(1,128)S(1)} %get-tuple-element.703), channel_id=1, source_target_pairs={{0,1},{1,2},{2,3},{4,5},{5,6},{6,7},{8,9},{9,10},{10,11},{12,13},{... | collective-permute-start | bytes 152 | tf_op jit(solution)/shard_map/ppermute | solution.py:31
  45.3 5.3 %fusion.51 = bf16[32,641,128]{2,1,0:T(8,128)(2,1)} fusion(bf16[32,1,1]{2,1,0:T(2,128)(2,1)S(1)} %copy.38, bf16[32,640,128]{2,1,0:T(8,128)(2,1)} %bitcast.75), kind=kLoop, calls=%fused_computation.70 | loop fusion | flops 15753216 | bytes 10494016 | tf_op jit(solution)/shard_map/concatenate | solution.py:173
  51.9 55.4 %collective-permute-done.1 = f32[4,12,256]{1,0,2:T(4,128)S(1)} collective-permute-done((f32[4,12,256]{1,0,2:T(4,128)}, f32[4,12,256]{1,0,2:T(4,128)S(1)}, u32[]{:S(2)}, u32[]{:S(2)}) %collective-permute-start.1) | collective-permute-done | bytes 49184 | tf_op jit(solution)/shard_map/ppermute | solution.py:23
  107.5 3.5 %collective-permute-start.3 = (f32[4,280,12]{1,0,2:T(4,128)S(1)}, f32[4,280,12]{1,0,2:T(4,128)S(1)}, u32[]{:S(2)}, u32[]{:S(2)}) collective-permute-start(f32[4,280,12]{1,0,2:T(4,128)S(1)} %get-tuple-element.678), channel_id=1, source_target_pairs={{1,0},{2,1},{3,2},{5,4},{6,5},{7,6},{9,8},{10,9},{11,10},{13,12},{... | collective-permute-start | bytes 161288 | tf_op jit(solution)/shard_map/ppermute | solution.py:32
  111.0 5.3 %collective-permute-start.2 = (f32[4,280,12]{1,0,2:T(4,128)S(1)}, f32[4,280,12]{1,0,2:T(4,128)S(1)}, u32[]{:S(2)}, u32[]{:S(2)}) collective-permute-start(f32[4,280,12]{1,0,2:T(4,128)S(1)} %get-tuple-element.677), channel_id=1, source_target_pairs={{0,1},{1,2},{2,3},{4,5},{5,6},{6,7},{8,9},{9,10},{10,11},{12,13},{... | collective-permute-start | bytes 161288 | tf_op jit(solution)/shard_map/ppermute | solution.py:31
  117.5 2.1 pad_maximum_fusion
  124.1 5.0 %while.72 = (s32[]{:T(128)}, f32[280,280]{1,0:T(8,128)S(1)}, f32[280,280]{1,0:T(8,128)S(1)}, f32[280,280]{1,0:T(8,128)S(1)}, f32[1,280]{1,0:T(1,128)S(1)}, /*ind...) while((s32[]{:T(128)}, f32[280,280]{1,0:T(8,128)S(1)}, f32[280,280]{1,0:T(8,128)S(1)}, ...), condition=%wide.region_1.0_spmd.clone, body=%wide.region_0.0_spmd.clone.sunk | while | flops 2117922 | bytes 10980301 | solution.py:198
  129.2 6.3 %all-to-all-start.1 = ((bf16[32,641,128]{2,1,0:T(8,128)(2,1)}), bf16[32,641,128]{2,1,0:T(8,128)(2,1)}, u32[]{:S(2)}, u32[]{:S(2)}) async-start(bf16[32,641,128]{2,1,0:T(8,128)(2,1)} %fusion.51), calls=%async_computation.1 | async-start | bytes 10616832 | tf_op jit(solution)/shard_map/all_to_all | solution.py:176
  135.6 12.6 %while.73 = (s32[]{:T(128)}, f32[280,280]{1,0:T(8,128)S(1)}, f32[280,280]{1,0:T(8,128)S(1)}, f32[280,280]{1,0:T(8,128)S(1)}, f32[1,280]{1,0:T(1,128)S(1)}, /*ind...) while((s32[]{:T(128)}, f32[280,280]{1,0:T(8,128)S(1)}, f32[280,280]{1,0:T(8,128)S(1)}, ...), condition=%wide.region_3.4_spmd.clone, body=%wide.region_2.3_spmd.clone.sunk | while | flops 2117922 | bytes 10980301 | solution.py:198
  154.5 5.3 %shard_map.82 = f32[4,3,128,128]{3,2,1,0:T(8,128)} custom-call(s32[32]{0:T(128)} %get-tuple-element.702.index_ref, s32[32]{0:T(128)} %get-tuple-element.700.valid_ref, f32[32]{0:T(128)} %fusion.65.scale_ref, f32[15]{0:T(128)} %reshape.145.weight_ref, f32[4,3,128,128]{3,2,1,0:T(8,128)} %fusion.62.spread_ref, bf16[32,641,128]{2,1,0:T(8,128)(2,1)} %all-to-all-done.innov_ref), custom_call_target="tpu_custom_call" | custom-call | tf_op jit(solution)/shard_map/pallas_call | solution.py:122
  162.7 5.9 %collective-permute-start.7 = (f32[3,12,256]{2,1,0:T(8,128)S(1)}, f32[3,12,256]{2,1,0:T(8,128)S(1)}, u32[]{:S(2)}, u32[]{:S(2)}) collective-permute-start(f32[3,12,256]{2,1,0:T(8,128)S(1)} %get-tuple-element.698), channel_id=1, source_target_pairs={{4,0},{8,4},{12,8},{16,12},{20,16},{24,20},{28,24},{32,28},{36,32}... | collective-permute-start | bytes 110600 | tf_op jit(solution)/shard_map/ppermute | solution.py:23
  168.6 35.0 %all-to-all-done.1.innov_ref = bf16[32,641,128]{2,1,0:T(8,128)(2,1)} async-done(((bf16[32,641,128]{2,1,0:T(8,128)(2,1)}), bf16[32,641,128]{2,1,0:T(8,128)(2,1)}, u32[]{:S(2)}, u32[]{:S(2)}) %all-to-all-start.1) | async-done | bytes 5251104 | tf_op jit(solution)/shard_map/all_to_all | solution.py:176
  205.3 5.3 %shard_map.83 = f32[4,3,128,128]{3,2,1,0:T(8,128)} custom-call(s32[32]{0:T(128)} %get-tuple-element.701.index_ref, s32[32]{0:T(128)} %get-tuple-element.699.valid_ref, f32[32]{0:T(128)} %fusion.64.scale_ref, f32[15]{0:T(128)} %reshape.145.weight_ref, f32[4,3,128,128]{3,2,1,0:T(8,128)} %fusion.58.spread_ref, bf16[32,641,128]{2,1,0:T(8,128)(2,1)} %all-to-all-done.1.innov_ref), custom_call_target="tpu_custom_call" | custom-call | tf_op jit(solution)/shard_map/pallas_call | solution.py:122
  213.6 2.0 collective-permute-start.11
  218.4 5.1 %collective-permute-start.8 = (f32[3,280,12]{2,1,0:T(8,128)S(1)}, f32[3,280,12]{2,1,0:T(8,128)S(1)}, u32[]{:S(2)}, u32[]{:S(2)}) collective-permute-start(f32[3,280,12]{2,1,0:T(8,128)S(1)} %get-tuple-element.693), channel_id=1, source_target_pairs={{0,1},{1,2},{2,3},{4,5},{5,6},{6,7},{8,9},{9,10},{10,11},{12,13},{... | collective-permute-start | bytes 120968 | tf_op jit(solution)/shard_map/ppermute | solution.py:31
  226.6 5.1 %collective-permute-start.12 = (f32[3,280,12]{2,1,0:T(8,128)}, f32[3,280,12]{2,1,0:T(8,128)}, u32[]{:S(2)}, u32[]{:S(2)}) collective-permute-start(f32[3,280,12]{2,1,0:T(8,128)} %get-tuple-element.691), channel_id=1, source_target_pairs={{0,1},{1,2},{2,3},{4,5},{5,6},{6,7},{8,9},{9,10},{10,11},{12,13},{... | collective-permute-start | bytes 120968 | tf_op jit(solution)/shard_map/ppermute | solution.py:31
  232.5 4.7 %while.74 = (s32[]{:T(128)}, f32[280,280]{1,0:T(8,128)S(1)}, f32[280,280]{1,0:T(8,128)S(1)}, f32[280,280]{1,0:T(8,128)S(1)}, f32[1,280]{1,0:T(1,128)S(1)}, /*ind...) while((s32[]{:T(128)}, f32[280,280]{1,0:T(8,128)S(1)}, f32[280,280]{1,0:T(8,128)S(1)}, ...), condition=%wide.region_5.6_spmd.clone, body=%wide.region_4.5_spmd.clone.sunk | while | flops 2196322 | bytes 10667821 | solution.py:213
  239.3 4.8 %while.75 = (s32[]{:T(128)}, f32[280,280]{1,0:T(8,128)S(1)}, f32[280,280]{1,0:T(8,128)S(1)}, f32[280,280]{1,0:T(8,128)S(1)}, f32[1,280]{1,0:T(1,128)S(1)}, /*ind...) while((s32[]{:T(128)}, f32[280,280]{1,0:T(8,128)S(1)}, f32[280,280]{1,0:T(8,128)S(1)}, ...), condition=%wide.region_7.8_spmd.clone, body=%wide.region_6.7_spmd.clone.sunk | while | flops 2196322 | bytes 10667821 | solution.py:213
  244.5 2.1 maximum_add_fusion
  (252 shorter events, 59.9 us)
Async XLA Ops:
  0.0 150.5 %copy-start = (bf16[128,128]{1,0:T(8,128)(2,1)S(1)}, bf16[128,128]{1,0:T(8,128)(2,1)}, u32[]{:S(2)}) copy-start(bf16[128,128]{1,0:T(8,128)(2,1)} %param.23) | copy-start | bytes 98308
  18.9 9.5 %copy-start.2 = (f32[3,256,256]{2,1,0:T(8,128)S(1)}, f32[3,256,256]{2,1,0:T(8,128)}, u32[]{:S(2)}) copy-start(f32[3,256,256]{2,1,0:T(8,128)} %param.20) | copy-start | bytes 2359300
  18.9 9.9 %copy-start.3 = (f32[256,256]{1,0:T(8,128)S(1)}, f32[256,256]{1,0:T(8,128)}, u32[]{:S(2)}) copy-start(f32[256,256]{1,0:T(8,128)} %param.21) | copy-start | bytes 786436
  18.9 110.4 %all-to-all-start = ((bf16[32,641,128]{2,1,0:T(8,128)(2,1)}), bf16[32,641,128]{2,1,0:T(8,128)(2,1)}, u32[]{:S(2)}, u32[]{:S(2)}) async-start(bf16[32,641,128]{2,1,0:T(8,128)(2,1)} %fusion.50), calls=%async_computation | async-start | bytes 10616832 | tf_op jit(solution)/shard_map/all_to_all | solution.py:176
  28.3 7.7 %copy-start.6 = (f32[256]{0:T(256)S(1)}, f32[256]{0:T(256)}, u32[]{:S(2)}) copy-start(f32[256]{0:T(256)} %param.22) | copy-start | bytes 3076
  28.3 16.3 %copy-start.7 = (s32[2,1,1,32]{3,2,1,0:T(1,128)S(1)}, s32[2,1,1,32]{3,2,1,0:T(1,128)}, u32[]{:S(2)}) copy-start(s32[2,1,1,32]{3,2,1,0:T(1,128)} %param.25) | copy-start | bytes 772
  30.5 76.7 %collective-permute-start.1 = (f32[4,12,256]{1,0,2:T(4,128)}, f32[4,12,256]{1,0,2:T(4,128)S(1)}, u32[]{:S(2)}, u32[]{:S(2)}) collective-permute-start(f32[4,12,256]{1,0,2:T(4,128)} %get-tuple-element.684), channel_id=1, source_target_pairs={{4,0},{8,4},{12,8},{16,12},{20,16},{24,20},{28,24},{32,28},{36,32}... | collective-permute-start | bytes 147464 | tf_op jit(solution)/shard_map/ppermute | solution.py:23
  36.0 71.3 %collective-permute-start = (f32[4,12,256]{1,0,2:T(4,128)S(1)}, f32[4,12,256]{1,0,2:T(4,128)S(1)}, u32[]{:S(2)}, u32[]{:S(2)}) collective-permute-start(f32[4,12,256]{1,0,2:T(4,128)S(1)} %get-tuple-element.683), channel_id=1, source_target_pairs={{0,4},{4,8},{8,12},{12,16},{16,20},{20,24},{24,28},{28,32},{32,36}... | collective-permute-start | bytes 147464 | tf_op jit(solution)/shard_map/ppermute | solution.py:22
  36.1 80.2 %collective-permute-start.5 = (f32[1,12]{1,0:T(1,128)S(1)}, f32[1,12]{1,0:T(1,128)S(1)}, u32[]{:S(2)}, u32[]{:S(2)}) collective-permute-start(f32[1,12]{1,0:T(1,128)S(1)} %get-tuple-element.704), channel_id=1, source_target_pairs={{1,0},{2,1},{3,2},{5,4},{6,5},{7,6},{9,8},{10,9},{11,10},{13,12},{... | collective-permute-start | bytes 152 | tf_op jit(solution)/shard_map/ppermute | solution.py:32
  39.5 76.8 %collective-permute-start.4 = (f32[1,12]{1,0:T(1,128)S(1)}, f32[1,12]{1,0:T(1,128)S(1)}, u32[]{:S(2)}, u32[]{:S(2)}) collective-permute-start(f32[1,12]{1,0:T(1,128)S(1)} %get-tuple-element.703), channel_id=1, source_target_pairs={{0,1},{1,2},{2,3},{4,5},{5,6},{6,7},{8,9},{9,10},{10,11},{12,13},{... | collective-permute-start | bytes 152 | tf_op jit(solution)/shard_map/ppermute | solution.py:31
  45.3 5.8 %copy-start.8 = (f32[5,3]{0,1:T(4,128)S(1)}, f32[5,3]{0,1:T(4,128)}, u32[]{:S(2)}) copy-start(f32[5,3]{0,1:T(4,128)} %param.24) | copy-start | bytes 184
  107.5 8.9 %collective-permute-start.3 = (f32[4,280,12]{1,0,2:T(4,128)S(1)}, f32[4,280,12]{1,0,2:T(4,128)S(1)}, u32[]{:S(2)}, u32[]{:S(2)}) collective-permute-start(f32[4,280,12]{1,0,2:T(4,128)S(1)} %get-tuple-element.678), channel_id=1, source_target_pairs={{1,0},{2,1},{3,2},{5,4},{6,5},{7,6},{9,8},{10,9},{11,10},{13,12},{... | collective-permute-start | bytes 161288 | tf_op jit(solution)/shard_map/ppermute | solution.py:32
  111.0 6.5 %collective-permute-start.2 = (f32[4,280,12]{1,0,2:T(4,128)S(1)}, f32[4,280,12]{1,0,2:T(4,128)S(1)}, u32[]{:S(2)}, u32[]{:S(2)}) collective-permute-start(f32[4,280,12]{1,0,2:T(4,128)S(1)} %get-tuple-element.677), channel_id=1, source_target_pairs={{0,1},{1,2},{2,3},{4,5},{5,6},{6,7},{8,9},{9,10},{10,11},{12,13},{... | collective-permute-start | bytes 161288 | tf_op jit(solution)/shard_map/ppermute | solution.py:31
  129.2 74.4 %all-to-all-start.1 = ((bf16[32,641,128]{2,1,0:T(8,128)(2,1)}), bf16[32,641,128]{2,1,0:T(8,128)(2,1)}, u32[]{:S(2)}, u32[]{:S(2)}) async-start(bf16[32,641,128]{2,1,0:T(8,128)(2,1)} %fusion.51), calls=%async_computation.1 | async-start | bytes 10616832 | tf_op jit(solution)/shard_map/all_to_all | solution.py:176
  162.7 52.9 %collective-permute-start.7 = (f32[3,12,256]{2,1,0:T(8,128)S(1)}, f32[3,12,256]{2,1,0:T(8,128)S(1)}, u32[]{:S(2)}, u32[]{:S(2)}) collective-permute-start(f32[3,12,256]{2,1,0:T(8,128)S(1)} %get-tuple-element.698), channel_id=1, source_target_pairs={{4,0},{8,4},{12,8},{16,12},{20,16},{24,20},{28,24},{32,28},{36,32}... | collective-permute-start | bytes 110600 | tf_op jit(solution)/shard_map/ppermute | solution.py:23
  168.6 47.0 %collective-permute-start.6 = (f32[3,12,256]{2,1,0:T(8,128)S(1)}, f32[3,12,256]{2,1,0:T(8,128)S(1)}, u32[]{:S(2)}, u32[]{:S(2)}) collective-permute-start(f32[3,12,256]{2,1,0:T(8,128)S(1)} %get-tuple-element.697), channel_id=1, source_target_pairs={{0,4},{4,8},{8,12},{12,16},{16,20},{20,24},{24,28},{28,32},{32,36}... | collective-permute-start | bytes 110600 | tf_op jit(solution)/shard_map/ppermute | solution.py:22
  213.5 10.1 %copy-start.1 = (f32[3,256,256]{2,1,0:T(8,128)}, f32[3,256,256]{2,1,0:T(8,128)S(1)}, u32[]{:S(2)}) copy-start(f32[3,256,256]{2,1,0:T(8,128)S(1)} %reshape.150) | copy-start | bytes 2359300
  213.6 10.0 %collective-permute-start.11 = (f32[3,12,256]{2,1,0:T(8,128)S(1)}, f32[3,12,256]{2,1,0:T(8,128)S(1)}, u32[]{:S(2)}, u32[]{:S(2)}) collective-permute-start(f32[3,12,256]{2,1,0:T(8,128)S(1)} %get-tuple-element.696), channel_id=1, source_target_pairs={{4,0},{8,4},{12,8},{16,12},{20,16},{24,20},{28,24},{32,28},{36,32}... | collective-permute-start | bytes 110600 | tf_op jit(solution)/shard_map/ppermute | solution.py:23
  215.6 8.0 %collective-permute-start.10 = (f32[3,12,256]{2,1,0:T(8,128)S(1)}, f32[3,12,256]{2,1,0:T(8,128)S(1)}, u32[]{:S(2)}, u32[]{:S(2)}) collective-permute-start(f32[3,12,256]{2,1,0:T(8,128)S(1)} %get-tuple-element.695), channel_id=1, source_target_pairs={{0,4},{4,8},{8,12},{12,16},{16,20},{20,24},{24,28},{28,32},{32,36}... | collective-permute-start | bytes 110600 | tf_op jit(solution)/shard_map/ppermute | solution.py:22
  216.3 15.5 %copy-start.5 = (f32[3,12,256]{2,1,0:T(8,128)S(1)}, f32[3,12,256]{2,1,0:T(8,128)}, u32[]{:S(2)}) copy-start(f32[3,12,256]{2,1,0:T(8,128)} %copy-done.4) | copy-start | bytes 110596
  216.5 15.3 %collective-permute-start.9 = (f32[3,280,12]{2,1,0:T(8,128)S(1)}, f32[3,280,12]{2,1,0:T(8,128)S(1)}, u32[]{:S(2)}, u32[]{:S(2)}) collective-permute-start(f32[3,280,12]{2,1,0:T(8,128)S(1)} %get-tuple-element.694), channel_id=1, source_target_pairs={{1,0},{2,1},{3,2},{5,4},{6,5},{7,6},{9,8},{10,9},{11,10},{13,12},{... | collective-permute-start | bytes 120968 | tf_op jit(solution)/shard_map/ppermute | solution.py:32
  218.4 13.4 %collective-permute-start.8 = (f32[3,280,12]{2,1,0:T(8,128)S(1)}, f32[3,280,12]{2,1,0:T(8,128)S(1)}, u32[]{:S(2)}, u32[]{:S(2)}) collective-permute-start(f32[3,280,12]{2,1,0:T(8,128)S(1)} %get-tuple-element.693), channel_id=1, source_target_pairs={{0,1},{1,2},{2,3},{4,5},{5,6},{6,7},{8,9},{9,10},{10,11},{12,13},{... | collective-permute-start | bytes 120968 | tf_op jit(solution)/shard_map/ppermute | solution.py:31
  224.7 12.5 %collective-permute-start.13 = (f32[3,280,12]{2,1,0:T(8,128)}, f32[3,280,12]{2,1,0:T(8,128)}, u32[]{:S(2)}, u32[]{:S(2)}) collective-permute-start(f32[3,280,12]{2,1,0:T(8,128)} %get-tuple-element.692), channel_id=1, source_target_pairs={{1,0},{2,1},{3,2},{5,4},{6,5},{7,6},{9,8},{10,9},{11,10},{13,12},{... | collective-permute-start | bytes 120968 | tf_op jit(solution)/shard_map/ppermute | solution.py:32
  226.6 10.6 %collective-permute-start.12 = (f32[3,280,12]{2,1,0:T(8,128)}, f32[3,280,12]{2,1,0:T(8,128)}, u32[]{:S(2)}, u32[]{:S(2)}) collective-permute-start(f32[3,280,12]{2,1,0:T(8,128)} %get-tuple-element.691), channel_id=1, source_target_pairs={{0,1},{1,2},{2,3},{4,5},{5,6},{6,7},{8,9},{9,10},{10,11},{12,13},{... | collective-permute-start | bytes 120968 | tf_op jit(solution)/shard_map/ppermute | solution.py:31
  (1 other events, 0.6 us)
